TPU v7x, 32 devices: a whole 2x2x4 slice. The times are simulated.
32 devices in a mesh: cell: 4 (over y, x), blk: 8 (over z, core).
Axes of the slice: x: 2, y: 2, z: 4, core: 2. Of those that a mesh axis runs over, the one named last changes fastest.
Arguments:
- codes: bfloat16 [16384, 128], P(('cell', 'blk')), may hold values from -60 to 60
- scales: float32 [16384], P(('cell', 'blk')), may hold values from 0.5 to 2
- coarse_ids: int32 [16384], P(('cell', 'blk')), may hold values from 0 to 3, as said below
- centroids: bfloat16 [32768, 128], P(('cell', 'blk')), may hold values from -6 to 6
Outputs:
- reconstruction: bfloat16 [16384, 128], P(('cell', 'blk'))
- residual: bfloat16 [16384, 128], P(('cell', 'blk'))
Inputs may be any that keep to these rules, and one draw needn't show every extreme that they name: `coarse_ids`: on every device, the number of its 512 rows that name partition g is the same for all devices; at most 256 rows of one device name one partition, and one partition is named by exactly 256 rows of every device.
All inputs are finite; a program needn't handle non-finite values.
Results may differ from a plain program's by a relative error of at most 0.006.
Values may be sent and summed in bfloat16 or wider, within the bound.
No kernel may reach another device: no remote copies, remote signals or barrier semaphores. Data moves between devices by JAX's collectives and lax.ppermute only.
A program may use at most 256 MiB of HBM per device.

v0:
```python
import math

import jax
import jax.numpy as jnp
from jax import lax
from jax.sharding import PartitionSpec as P


def local(codes, scales, coarse_ids, centroids):
    rows_dev = codes.shape[0]
    width = codes.shape[1]
    loops = lax.axis_size("cell")
    cap = 2 * rows_dev // loops
    beta = 1.0 / math.sqrt(width)
    dequant = (codes.astype(jnp.float32) * scales[:, None]).astype(jnp.bfloat16)
    onehot = (coarse_ids[:, None] == jnp.arange(loops, dtype=jnp.int32)[None, :]).astype(jnp.int32)
    ranks = jnp.sum(jnp.cumsum(onehot, axis=0) * onehot, axis=1) - 1
    slots = coarse_ids * cap + ranks
    outgoing = jnp.zeros((loops * cap, width), jnp.bfloat16).at[slots].set(dequant)
    arrived = lax.all_to_all(
        outgoing.reshape(loops, cap, width), "cell", split_axis=0, concat_axis=0, tiled=True
    )
    queries = arrived.reshape(loops * cap, width)

    def scores_of(piece):
        product = lax.dot_general(
            queries, piece, (((1,), (1,)), ((), ())), preferred_element_type=jnp.float32
        )
        return product * beta

    top = jnp.max(scores_of(lax.all_gather(centroids, "blk", axis=0, tiled=True)), axis=1)
    piece = lax.all_gather(centroids, "blk", axis=0, tiled=True)
    weights = jnp.exp(scores_of(piece) - top[:, None]).astype(jnp.bfloat16)
    total = jnp.sum(weights.astype(jnp.float32), axis=1)
    numer = jnp.dot(weights, piece, preferred_element_type=jnp.float32)
    total, numer = (total, numer)
    recon = (numer / total[:, None]).astype(jnp.bfloat16)
    remote_residual = (queries.astype(jnp.float32) - recon.astype(jnp.float32)).astype(jnp.bfloat16)
    stacked = jnp.stack([recon, remote_residual]).reshape(2, loops, cap, width)
    back = lax.all_to_all(stacked, "cell", split_axis=1, concat_axis=1, tiled=True).reshape(
        2, loops * cap, width
    )
    return (back[0][slots], back[1][slots])


def solution(mesh):
    in_specs = (
        P(("cell", "blk"), None),
        P(("cell", "blk")),
        P(("cell", "blk")),
        P(("cell", "blk"), None),
    )
    out_specs = (P(("cell", "blk"), None), P(("cell", "blk"), None))
    return jax.shard_map(local, mesh=mesh, in_specs=in_specs, out_specs=out_specs, check_vma=False)
```

profile of v0, /device:TPU:0, one launch (start us, length us, event | category | flops | bytes accessed | tf_op | source)
XLA Modules:
  0.0 99.3 jit_solution(16947095340633523881)
XLA Ops:
  7.2 0.0 all-gather.2.cloned.1.call-start
  7.2 0.7 all-gather.2.cloned.1.call-update
  7.9 0.7 fusion.6
  8.6 1.2 %reduce-window.6 = s32[4,4,128]{2,1,0:T(4,128)S(1)} reduce-window(s32[4,4,128]{2,1,0:T(4,128)S(1)} %fusion.6, s32[]{:T(128)} %constant.4.clone.1), window={size=1x1x128 pad=0_0x0_0x127_0}, to_apply=%region_0.0 | reduce-window | flops 260096 | bytes 16388 | tf_op jit(solution)/shard_map/reduce-window
  9.8 0.2 slice_reduce_fusion
  10.0 0.2 reduce-window.9
  10.2 0.1 add_bitcast_fusion
  10.3 0.7 fusion.5
  11.0 0.7 compare_select_fusion
  11.7 2.3 %scatter_custom_fusion = bf16[1024,128]{1,0:T(8,128)(2,1)S(1)} fusion(s32[512]{0:T(512)S(1)} %compare_select_fusion, bf16[512,128]{1,0:T(8,128)(2,1)} %param.4, f32[512]{0:T(512)} %param.5, bf16[]{:T(256)} %constant.8.clone.1), kind=kCustom, calls=%fused_computation.11 | custom fusion | flops 196608 | bytes 395266 | tf_op jit(solution)/shard_map/scatter | solution.py:19
  14.0 10.7 %all_to_all.10 = bf16[4,256,128]{2,1,0:T(8,128)(2,1)S(1)} all-to-all(bf16[4,256,128]{2,1,0:T(8,128)(2,1)S(1)} %bitcast.34), channel_id=1, replica_groups=mesh['cell'=4,'blk'=8] {'cell'}, dimensions={0} | all-to-all | bytes 524288 | tf_op jit(solution)/shard_map/all_to_all | solution.py:20
  24.7 16.8 %all-gather.2.cloned.1.call-done = bf16[8192,128]{1,0:T(8,128)(2,1)} async-done(((bf16[1024,128]{1,0:T(8,128)(2,1)}), bf16[8192,128]{1,0:T(8,128)(2,1)}) %all-gather.2.cloned.1.call-update) | async-done | bytes 2097168 | tf_op jit(solution)/shard_map/all_gather | solution.py:32
  41.5 14.6 %multiply_reduce_fusion = (f32[1024]{0:T(1024)S(1)}, f32[1024,8192]{1,0:T(8,128)}) fusion(bf16[1024,128]{1,0:T(8,128)(2,1)S(1)} %bitcast.33, bf16[8192,128]{1,0:T(8,128)(2,1)} %all-gather.2.cloned.1.call-done), kind=kOutput, calls=%fused_computation.5 | convolution fusion | flops 2164259840 | bytes 35917824 | tf_op jit(solution)/shard_map/dot_general | solution.py:26
  56.1 0.0 copy-start
  56.1 15.0 %convert_reduce_fusion = (f32[1024]{0:T(1024)S(1)}, bf16[1024,8192]{1,0:T(8,128)(2,1)S(1)}) fusion(f32[1024]{0:T(1024)S(1)} %get-tuple-element.6, f32[1024,8192]{1,0:T(8,128)} %get-tuple-element.7), kind=kLoop, calls=%fused_computation.3 | loop fusion | flops 41942016 | bytes 50339840 | tf_op jit(solution)/shard_map/reduce_sum | solution.py:34
  71.1 0.0 copy-done
  71.1 4.5 %subtract_convert_fusion = (bf16[1024,128]{1,0:T(8,128)(2,1)S(1)}, bf16[1024,128]{1,0:T(8,128)(2,1)S(1)}) fusion(bf16[4,256,128]{2,1,0:T(8,128)(2,1)S(1)} %all_to_all.10, f32[1024]{0:T(1024)S(1)} %get-tuple-element.2, bf16[1024,8192]{1,0:T(8,128)(2,1)S(1)} %get-tuple-element.3, bf16[8192,128]{1,0:T(8,128)(2,1)S(1)} %copy-done), kind=kOutput, calls=%fused_computation.9 | convolution fusion | flops 2148270080 | bytes 19664896 | tf_op jit(solution)/shard_map/dot_general | solution.py:35
  75.6 0.8 pad_maximum_fusion
  76.4 3.6 %all-to-all-start.1 = ((bf16[2,4,256,128]{3,2,0,1:T(8,128)(2,1)}), bf16[2,4,256,128]{3,2,0,1:T(8,128)(2,1)S(1)}, u32[]{:S(2)}, u32[]{:S(2)}) async-start(bf16[2,4,256,128]{3,2,0,1:T(8,128)(2,1)} %pad_maximum_fusion), calls=%async_computation.1 | async-start | bytes 1048576 | tf_op jit(solution)/shard_map/all_to_all | solution.py:40
  80.1 8.5 %all-to-all-done.1 = bf16[2,4,256,128]{3,2,0,1:T(8,128)(2,1)S(1)} async-done(((bf16[2,4,256,128]{3,2,0,1:T(8,128)(2,1)}), bf16[2,4,256,128]{3,2,0,1:T(8,128)(2,1)S(1)}, u32[]{:S(2)}, u32[]{:S(2)}) %all-to-all-start.1) | async-done | bytes 524320 | tf_op jit(solution)/shard_map/all_to_all | solution.py:40
  88.6 1.9 %gather_fusion.1 = bf16[512,128]{1,0:T(8,128)(2,1)} fusion(bf16[1024,128]{1,0:T(8,128)(2,1)S(1)} %bitcast.32, s32[1024]{0:T(1024)S(1)} %pad_clamp_fusion), kind=kCustom, calls=%fused_computation.1 | custom fusion | bytes 264192 | tf_op jit(solution)/shard_map/gather | solution.py:43
  90.5 1.9 %gather_fusion = bf16[512,128]{1,0:T(8,128)(2,1)} fusion(bf16[1024,128]{1,0:T(8,128)(2,1)S(1)} %bitcast.31, s32[1024]{0:T(1024)S(1)} %pad_clamp_fusion), kind=kCustom, calls=%fused_computation | custom fusion | bytes 264192 | tf_op jit(solution)/shard_map/gather | solution.py:43
  (2 shorter events, 0.0 us)
Async XLA Ops:
  7.2 34.3 %all-gather.2.cloned.1.call-start = ((), (), s32[]{:S(2)}) async-start(), calls=%async_computation.2 | async-start | bytes 2359296 | tf_op jit(solution)/shard_map/all_gather | solution.py:32
  56.1 15.0 %copy-start = (bf16[8192,128]{1,0:T(8,128)(2,1)S(1)}, bf16[8192,128]{1,0:T(8,128)(2,1)}, u32[]{:S(2)}) copy-start(bf16[8192,128]{1,0:T(8,128)(2,1)} %all-gather.2.cloned.1.call-done) | copy-start | bytes 6291460
  76.4 12.1 %all-to-all-start.1 = ((bf16[2,4,256,128]{3,2,0,1:T(8,128)(2,1)}), bf16[2,4,256,128]{3,2,0,1:T(8,128)(2,1)S(1)}, u32[]{:S(2)}, u32[]{:S(2)}) async-start(bf16[2,4,256,128]{3,2,0,1:T(8,128)(2,1)} %pad_maximum_fusion), calls=%async_computation.1 | async-start | bytes 1048576 | tf_op jit(solution)/shard_map/all_to_all | solution.py:40
Sparse Core Ops, SparseCore 0:
  9.6 31.8 all-gather.1
where the time goes:
time: 99.7 us; the launch traced here: 99.3 us
  waiting for transfers between devices  26 us (26%)
  other arithmetic  21.6 us (22%)
  matrix products  19.1 us (19%)
  between operations  14.1 us (14%)
  blocking collectives  10.7 us (11%)
  local copies, waits for them, and re-layouts  4.08 us (4%)
  starting transfers between devices  3.69 us (4%)
    all_gather x1, waiting for transfers between devices, local(): piece = lax.all_gather(centroids, 'blk', axis=0, tiled=True)  16.8 us
    reduce_sum x1, other arithmetic, local(): total = jnp.sum(weights.astype(jnp.float32), axis=1)  15 us
    dot_general x1, matrix products, scores_of(): lax.dot_general(queries, piece, (((1,), (1,)), ((), ())), preferred_eleme...  14.6 us
    all_to_all x1, blocking collectives, local(): lax.all_to_all(outgoing.reshape(loops, cap, width), 'cell', split_axis=0,...  10.7 us
    all_to_all x1, waiting for transfers between devices, local(): lax.all_to_all(stacked, 'cell', split_axis=1, concat_axis=1, tiled=True)  8.47 us
    dot_general x1, matrix products, local(): numer = jnp.dot(weights, piece, preferred_element_type=jnp.float32)  4.49 us
    gather x2, local copies, waits for them, and re-layouts, local(): return (back[0][slots], back[1][slots])  3.83 us
    all_to_all x1, starting transfers between devices, local(): lax.all_to_all(stacked, 'cell', split_axis=1, concat_axis=1, tiled=True)  3.65 us
  transfers between devices with their start and end apart: 2, of which 2 were waited for; matrix products, arithmetic and copies ran while one was open for 6% of the time, Pallas kernels for 0%

commit v1 on v0

v1 whole, which is shorter than its diff:
```python
import functools
import math

import jax
import jax.numpy as jnp
from jax import lax
from jax.experimental import pallas as pl
from jax.experimental.pallas import tpu as pltpu
from jax.sharding import Mesh
from jax.sharding import PartitionSpec as P

ROWS = ("cell", "chip", "core")


def _soft_kernel(q_ref, c_ref, o_ref, m_sc, l_sc, acc_sc, *, chunk, beta):
    n_chunks = c_ref.shape[0] // chunk
    q = q_ref[...]

    def scores(i):
        c = c_ref[pl.ds(pl.multiple_of(i * chunk, chunk), chunk), :]
        s = lax.dot_general(q, c, (((1,), (1,)), ((), ())), preferred_element_type=jnp.float32)
        return s * beta, c

    m_sc[...] = jnp.full(m_sc.shape, -jnp.inf, jnp.float32)

    @pl.loop(0, n_chunks)
    def _(i):
        s, _ = scores(i)
        m_sc[...] = jnp.maximum(m_sc[...], jnp.max(s, axis=1, keepdims=True))

    l_sc[...] = jnp.zeros(l_sc.shape, jnp.float32)
    acc_sc[...] = jnp.zeros(acc_sc.shape, jnp.float32)
    top = m_sc[...]

    @pl.loop(0, n_chunks)
    def _(i):
        s, c = scores(i)
        w = jnp.exp(s - top).astype(jnp.bfloat16)
        l_sc[...] += jnp.sum(w.astype(jnp.float32), axis=1, keepdims=True)
        acc_sc[...] += jnp.dot(w, c, preferred_element_type=jnp.float32)

    o_ref[...] = (acc_sc[...] / l_sc[...]).astype(o_ref.dtype)


def soft_reconstruct(queries, cents, *, tq=256, chunk=512):
    slots, width = queries.shape
    n_cent = cents.shape[0]
    beta = 1.0 / math.sqrt(width)
    flops = 3 * 2 * slots * n_cent * width
    return pl.pallas_call(
        functools.partial(_soft_kernel, chunk=chunk, beta=beta),
        out_shape=jax.ShapeDtypeStruct((slots, width), jnp.bfloat16),
        grid=(slots // tq,),
        in_specs=[
            pl.BlockSpec((tq, width), lambda i: (i, 0)),
            pl.BlockSpec((n_cent, width), lambda i: (0, 0)),
        ],
        out_specs=pl.BlockSpec((tq, width), lambda i: (i, 0)),
        scratch_shapes=[
            pltpu.VMEM((tq, 1), jnp.float32),
            pltpu.VMEM((tq, 1), jnp.float32),
            pltpu.VMEM((tq, width), jnp.float32),
        ],
        compiler_params=pltpu.CompilerParams(vmem_limit_bytes=48 * 1024 * 1024),
        cost_estimate=pl.CostEstimate(
            flops=flops,
            transcendentals=slots * n_cent,
            bytes_accessed=2 * (2 * slots * width + n_cent * width),
        ),
    )(queries, cents)


def local(codes, scales, coarse_ids, centroids):
    rows_dev = codes.shape[0]
    width = codes.shape[1]
    loops = lax.axis_size("cell")
    cap = 2 * rows_dev // loops
    dequant = (codes.astype(jnp.float32) * scales[:, None]).astype(jnp.bfloat16)
    onehot = (coarse_ids[:, None] == jnp.arange(loops, dtype=jnp.int32)[None, :]).astype(jnp.int32)
    ranks = jnp.sum(jnp.cumsum(onehot, axis=0) * onehot, axis=1) - 1
    slots = coarse_ids * cap + ranks
    outgoing = jnp.zeros((loops * cap, width), jnp.bfloat16).at[slots].set(dequant)
    arrived = lax.all_to_all(
        outgoing.reshape(loops, cap, width), "cell", split_axis=0, concat_axis=0, tiled=True
    )
    queries = arrived.reshape(loops * cap, width)
    part = lax.all_gather(centroids, "chip", axis=0, tiled=True)
    part = lax.all_gather(part, "core", axis=0, tiled=True)
    recon = soft_reconstruct(queries, part)
    back = lax.all_to_all(
        recon.reshape(loops, cap, width), "cell", split_axis=0, concat_axis=0, tiled=True
    ).reshape(loops * cap, width)
    mine = back[slots]
    residual = (dequant.astype(jnp.float32) - mine.astype(jnp.float32)).astype(jnp.bfloat16)
    return (mine, residual)


def solution(mesh):
    n_cell = mesh.shape["cell"]
    n_blk = mesh.shape["blk"]
    fine = Mesh(mesh.devices.reshape(n_cell, n_blk // 2, 2), ROWS)
    rows = P(ROWS, None)
    in_specs = (rows, P(ROWS), P(ROWS), rows)
    out_specs = (rows, rows)
    return jax.shard_map(local, mesh=fine, in_specs=in_specs, out_specs=out_specs, check_vma=False)
```

time: 99.7 us -> 122 us (1.22)
  Pallas kernels: 0 us -> 46.8 us
  matrix products: 19.1 us -> 0 us
  other arithmetic: 21.6 us -> 6.63 us
  waiting for transfers between devices: 26 us -> 38.4 us
  blocking collectives: 10.7 us -> 9.17 us
    pallas_call x0 -> x1, Pallas kernels: none -> 46.8 us  [soft_reconstruct(): pl.pallas_call(functools.partial(_soft_kernel, chunk=chunk, beta=beta), o...]
    dot_general x2 -> x0, matrix products: 19.1 us -> none  [the longest x1 14.6 us: scores_of(): lax.dot_general(queries, piece, (((1,), (1,)), ((), ())), preferred_eleme...]
    all_gather x1 -> x2, waiting for transfers between devices: 16.8 us -> 32.3 us  [the longest x1 32.3 us: local(): part = lax.all_gather(centroids, 'chip', axis=0, tiled=True)]
    reduce_sum x1 -> x0, other arithmetic: 15 us -> none  [local(): total = jnp.sum(weights.astype(jnp.float32), axis=1)]
    all_to_all x1, waiting for transfers between devices: 8.47 us -> 5.32 us  [local(): lax.all_to_all(recon.reshape(loops, cap, width), 'cell', split_axis=0, co...]
    gather x2 -> x1, local copies, waits for them, and re-layouts: 3.83 us -> 1.33 us  [local(): mine = back[slots]]
    unnamed x2 -> x8, local copies, waits for them, and re-layouts: 0.01 us -> 1.61 us
    all_to_all x1, blocking collectives: 10.7 us -> 9.17 us  [local(): lax.all_to_all(outgoing.reshape(loops, cap, width), 'cell', split_axis=0,...]
  transfers between devices with their start and end apart: 2 -> 3, of which waited for: 2 -> 2; matrix products, arithmetic and copies ran while one was open for 6% -> 5% of each run, Pallas kernels for 0% -> 0%
where the time goes in v1:
time: 122 us
  Pallas kernels  46.8 us (38%)
  waiting for transfers between devices  38.4 us (31%)
  between operations  14.1 us (12%)
  blocking collectives  9.17 us (8%)
  other arithmetic  6.63 us (5%)
  starting transfers between devices  3.48 us (3%)
  local copies, waits for them, and re-layouts  3.15 us (3%)
    pallas_call x1, Pallas kernels, soft_reconstruct(): pl.pallas_call(functools.partial(_soft_kernel, chunk=chunk, beta=beta), o...  46.8 us
    all_gather x1, waiting for transfers between devices, local(): part = lax.all_gather(centroids, 'chip', axis=0, tiled=True)  32.3 us
    all_to_all x1, blocking collectives, local(): lax.all_to_all(outgoing.reshape(loops, cap, width), 'cell', split_axis=0,...  9.17 us
    all_to_all x1, waiting for transfers between devices, local(): lax.all_to_all(recon.reshape(loops, cap, width), 'cell', split_axis=0, co...  5.32 us
    all_to_all x1, starting transfers between devices, local(): lax.all_to_all(recon.reshape(loops, cap, width), 'cell', split_axis=0, co...  3.4 us
  transfers between devices with their start and end apart: 3, of which 2 were waited for; matrix products, arithmetic and copies ran while one was open for 5% of the time, Pallas kernels for 0%

profile of v1, /device:TPU:0, one launch (start us, length us, event | category | flops | bytes accessed | tf_op | source)
XLA Modules:
  0.0 121.7 jit_solution(1143810953865279152)
XLA Ops:
  7.2 0.0 all-gather.3.cloned.1.call-start
  7.2 0.7 all-gather.3.cloned.1.call-update
  7.9 0.0 all-gather.5.cloned.1.call-start
  7.9 32.3 %all-gather.3.cloned.1.call-done = bf16[4096,128]{1,0:T(8,128)(2,1)} async-done(((bf16[1024,128]{1,0:T(8,128)(2,1)}), bf16[4096,128]{1,0:T(8,128)(2,1)}) %all-gather.3.cloned.1.call-update) | async-done | bytes 1048592 | tf_op jit(solution)/shard_map/all_gather | solution.py:87
  40.3 0.0 all-gather.5.cloned.1.call-update
  40.3 0.7 fusion.4
  41.0 1.2 reduce-window.6
  42.2 0.2 slice_reduce_fusion
  42.4 0.2 reduce-window.9
  42.6 0.1 add_bitcast_fusion
  42.7 0.7 fusion.3
  43.4 0.7 compare_select_fusion
  44.1 2.3 %scatter_custom_fusion = bf16[1024,128]{1,0:T(8,128)(2,1)S(1)} fusion(s32[512]{0:T(512)S(1)} %compare_select_fusion, bf16[]{:T(256)} %constant.5.clone.1, bf16[512,128]{1,0:T(8,128)(2,1)} %param.4, f32[512]{0:T(512)} %param.5), kind=kCustom, calls=%fused_computation.4 | custom fusion | flops 196608 | bytes 395266 | tf_op jit(solution)/shard_map/scatter | solution.py:82
  46.4 9.2 %all_to_all.10 = bf16[4,256,128]{2,1,0:T(8,128)(2,1)S(1)} all-to-all(bf16[4,256,128]{2,1,0:T(8,128)(2,1)S(1)} %bitcast.23), channel_id=1, replica_groups=mesh['cell'=4,'chip'=4,'core'=2] {'cell'}, dimensions={0} | all-to-all | bytes 524288 | tf_op jit(solution)/shard_map/all_to_all | solution.py:83
  55.5 0.0 all-gather.5.cloned.1.call-done.c_ref
  55.5 0.0 copy-start
  55.5 1.6 %copy-done = bf16[8192,128]{1,0:T(8,128)(2,1)S(1)} copy-done((bf16[8192,128]{1,0:T(8,128)(2,1)S(1)}, bf16[8192,128]{1,0:T(8,128)(2,1)}, u32[]{:S(2)}) %copy-start) | copy-done | bytes 2097176
  57.1 0.0 copy-start.2
  57.1 0.0 copy-start.3
  57.1 46.8 %shard_map.59 = bf16[1024,128]{1,0:T(8,128)(2,1)} custom-call(bf16[1024,128]{1,0:T(8,128)(2,1)S(1)} %bitcast.21, bf16[8192,128]{1,0:T(8,128)(2,1)S(1)} %copy-done), custom_call_target="tpu_custom_call" | custom-call | flops 6442450944 | bytes 2621440 | tf_op jit(solution)/shard_map/pallas_call | solution.py:50
  103.9 3.4 %all-to-all-start.1 = ((bf16[4,256,128]{2,1,0:T(8,128)(2,1)}), bf16[4,256,128]{2,1,0:T(8,128)(2,1)S(1)}, u32[]{:S(2)}, u32[]{:S(2)}) async-start(bf16[4,256,128]{2,1,0:T(8,128)(2,1)} %bitcast.4), calls=%async_computation.1 | async-start | bytes 524288 | tf_op jit(solution)/shard_map/all_to_all | solution.py:90
  107.4 5.3 %all-to-all-done.1 = bf16[4,256,128]{2,1,0:T(8,128)(2,1)S(1)} async-done(((bf16[4,256,128]{2,1,0:T(8,128)(2,1)}), bf16[4,256,128]{2,1,0:T(8,128)(2,1)S(1)}, u32[]{:S(2)}, u32[]{:S(2)}) %all-to-all-start.1) | async-done | bytes 262176 | tf_op jit(solution)/shard_map/all_to_all | solution.py:90
  112.7 1.3 %gather_fusion = bf16[512,128]{1,0:T(8,128)(2,1)S(1)} fusion(bf16[1024,128]{1,0:T(8,128)(2,1)S(1)} %bitcast.22, s32[1024]{0:T(1024)S(1)} %pad_clamp_fusion), kind=kCustom, calls=%fused_computation | custom fusion | bytes 264192 | tf_op jit(solution)/shard_map/gather | solution.py:93
  114.0 0.0 copy-done.2
  114.0 0.0 copy-done.3
  114.0 0.0 copy-start.1
  114.1 0.8 subtract_convert_fusion
  114.8 0.0 copy-done.1
  (1 shorter events, 0.0 us)
Async XLA Ops:
  7.2 33.1 %all-gather.3.cloned.1.call-start = ((), (), s32[]{:S(2)}) async-start(), calls=%async_computation.2 | async-start | bytes 1310720 | tf_op jit(solution)/shard_map/all_gather | solution.py:87
  7.9 47.6 %all-gather.5.cloned.1.call-start = ((), (), s32[]{:S(2)}) async-start(), calls=%async_computation.3 | async-start | bytes 3145728 | tf_op jit(solution)/shard_map/all_gather | solution.py:88
  55.5 1.6 %copy-start = (bf16[8192,128]{1,0:T(8,128)(2,1)S(1)}, bf16[8192,128]{1,0:T(8,128)(2,1)}, u32[]{:S(2)}) copy-start(bf16[8192,128]{1,0:T(8,128)(2,1)} %all-gather.5.cloned.1.call-done.c_ref) | copy-start | bytes 6291460
  57.1 56.9 %copy-start.2 = (bf16[512,128]{1,0:T(8,128)(2,1)S(1)}, bf16[512,128]{1,0:T(8,128)(2,1)}, u32[]{:S(2)}) copy-start(bf16[512,128]{1,0:T(8,128)(2,1)} %param.4) | copy-start | bytes 393220
  57.1 56.9 %copy-start.3 = (f32[512]{0:T(512)S(1)}, f32[512]{0:T(512)}, u32[]{:S(2)}) copy-start(f32[512]{0:T(512)} %param.5) | copy-start | bytes 6148
  103.9 8.8 %all-to-all-start.1 = ((bf16[4,256,128]{2,1,0:T(8,128)(2,1)}), bf16[4,256,128]{2,1,0:T(8,128)(2,1)S(1)}, u32[]{:S(2)}, u32[]{:S(2)}) async-start(bf16[4,256,128]{2,1,0:T(8,128)(2,1)} %bitcast.4), calls=%async_computation.1 | async-start | bytes 524288 | tf_op jit(solution)/shard_map/all_to_all | solution.py:90
  114.0 0.8 copy-start.1
Sparse Core Ops, SparseCore 0:
  9.5 30.6 all-gather.2
  41.8 9.9 all-gather.4

commit v2 on v1

v2 whole, which is shorter than its diff:
```python
import functools
import math

import jax
import jax.numpy as jnp
from jax import lax
from jax.experimental import pallas as pl
from jax.experimental.pallas import tpu as pltpu
from jax.sharding import PartitionSpec as P


def _soft_kernel(q_ref, c_ref, o_ref, m_sc, l_sc, acc_sc, s_sc, *, chunk, beta):
    n_chunks = c_ref.shape[0] // chunk
    lanes = m_sc.shape[1]
    q = q_ref[...]
    m_sc[...] = jnp.full(m_sc.shape, -jnp.inf, jnp.float32)

    @pl.loop(0, n_chunks)
    def _(i):
        cols = pl.ds(pl.multiple_of(i * chunk, chunk), chunk)
        s = lax.dot_general(
            q, c_ref[cols, :], (((1,), (1,)), ((), ())), preferred_element_type=jnp.float32
        ) * beta
        s_sc[:, cols] = s
        m = m_sc[...]
        for j in range(chunk // lanes):
            m = jnp.maximum(m, s[:, j * lanes:(j + 1) * lanes])
        m_sc[...] = m

    top = jnp.max(m_sc[...], axis=1, keepdims=True)
    l_sc[...] = jnp.zeros(l_sc.shape, jnp.float32)
    acc_sc[...] = jnp.zeros(acc_sc.shape, jnp.float32)

    @pl.loop(0, n_chunks)
    def _(i):
        cols = pl.ds(pl.multiple_of(i * chunk, chunk), chunk)
        w = jnp.exp(s_sc[:, cols] - top).astype(jnp.bfloat16)
        wf = w.astype(jnp.float32)
        l = l_sc[...]
        for j in range(chunk // lanes):
            l = l + wf[:, j * lanes:(j + 1) * lanes]
        l_sc[...] = l
        acc_sc[...] += jnp.dot(w, c_ref[cols, :], preferred_element_type=jnp.float32)

    total = jnp.sum(l_sc[...], axis=1, keepdims=True)
    o_ref[...] = (acc_sc[...] / total).astype(o_ref.dtype)


def soft_reconstruct(queries, cents):
    slots, width = queries.shape
    n_cent = cents.shape[0]
    chunk = min(2048, n_cent)
    tq = min(512, slots, (16 << 20) // (4 * n_cent))
    vmem = 4 * tq * n_cent + 2 * 2 * n_cent * width + 8 * tq * width * 4 + (8 << 20)
    return pl.pallas_call(
        functools.partial(_soft_kernel, chunk=chunk, beta=1.0 / math.sqrt(width)),
        out_shape=jax.ShapeDtypeStruct((slots, width), jnp.bfloat16),
        grid=(slots // tq,),
        in_specs=[
            pl.BlockSpec((tq, width), lambda i: (i, 0)),
            pl.BlockSpec((n_cent, width), lambda i: (0, 0)),
        ],
        out_specs=pl.BlockSpec((tq, width), lambda i: (i, 0)),
        scratch_shapes=[
            pltpu.VMEM((tq, 128), jnp.float32),
            pltpu.VMEM((tq, 128), jnp.float32),
            pltpu.VMEM((tq, width), jnp.float32),
            pltpu.VMEM((tq, n_cent), jnp.float32),
        ],
        compiler_params=pltpu.CompilerParams(vmem_limit_bytes=min(vmem, 60 << 20)),
        cost_estimate=pl.CostEstimate(
            flops=2 * 2 * slots * n_cent * width,
            transcendentals=slots * n_cent,
            bytes_accessed=2 * (2 * slots * width + n_cent * width),
        ),
    )(queries, cents)


def local(codes, scales, coarse_ids, centroids):
    rows_dev = codes.shape[0]
    width = codes.shape[1]
    loops = lax.axis_size("cell")
    cap = 2 * rows_dev // loops
    dequant = (codes.astype(jnp.float32) * scales[:, None]).astype(jnp.bfloat16)
    onehot = (coarse_ids[:, None] == jnp.arange(loops, dtype=jnp.int32)[None, :]).astype(jnp.int32)
    ranks = jnp.sum(jnp.cumsum(onehot, axis=0) * onehot, axis=1) - 1
    slots = coarse_ids * cap + ranks
    outgoing = jnp.zeros((loops * cap, width), jnp.bfloat16).at[slots].set(dequant)
    arrived = lax.all_to_all(
        outgoing.reshape(loops, cap, width), "cell", split_axis=0, concat_axis=0, tiled=True
    )
    queries = arrived.reshape(loops * cap, width)
    part = lax.all_gather(centroids, "blk", axis=0, tiled=True)
    recon = soft_reconstruct(queries, part)
    back = lax.all_to_all(
        recon.reshape(loops, cap, width), "cell", split_axis=0, concat_axis=0, tiled=True
    ).reshape(loops * cap, width)
    mine = back[slots]
    residual = (dequant.astype(jnp.float32) - mine.astype(jnp.float32)).astype(jnp.bfloat16)
    return (mine, residual)


def solution(mesh):
    rows = P(("cell", "blk"), None)
    in_specs = (rows, P(("cell", "blk")), P(("cell", "blk")), rows)
    out_specs = (rows, rows)
    return jax.shard_map(local, mesh=mesh, in_specs=in_specs, out_specs=out_specs, check_vma=False)
```

time: 122 us -> 76.6 us (0.63)
  Pallas kernels: 46.8 us -> 14.7 us
  waiting for transfers between devices: 38.4 us -> 23.2 us
  blocking collectives: 9.17 us -> 10.7 us
    pallas_call x1, Pallas kernels: 46.8 us -> 14.7 us  [soft_reconstruct(): pl.pallas_call(functools.partial(_soft_kernel, chunk=chunk, beta=1.0 / ma...]
    all_gather x2 -> x1, waiting for transfers between devices: 32.3 us -> 16.8 us  [local(): part = lax.all_gather(centroids, 'blk', axis=0, tiled=True)]
    all_to_all x1, blocking collectives: 9.17 us -> 10.7 us  [local(): lax.all_to_all(outgoing.reshape(loops, cap, width), 'cell', split_axis=0,...]
  transfers between devices with their start and end apart: 3 -> 2, of which waited for: 2 -> 2; matrix products, arithmetic and copies ran while one was open for 5% -> 8% of each run, Pallas kernels for 0% -> 0%
where the time goes in v2:
time: 76.6 us; the launch traced here: 76.2 us
  waiting for transfers between devices  23.2 us (30%)
  Pallas kernels  14.7 us (19%)
  between operations  14.1 us (18%)
  blocking collectives  10.7 us (14%)
  other arithmetic  6.63 us (9%)
  starting transfers between devices  3.68 us (5%)
  local copies, waits for them, and re-layouts  3.15 us (4%)
    all_gather x1, waiting for transfers between devices, local(): part = lax.all_gather(centroids, 'blk', axis=0, tiled=True)  16.8 us
    pallas_call x1, Pallas kernels, soft_reconstruct(): pl.pallas_call(functools.partial(_soft_kernel, chunk=chunk, beta=1.0 / ma...  14.7 us
    all_to_all x1, blocking collectives, local(): lax.all_to_all(outgoing.reshape(loops, cap, width), 'cell', split_axis=0,...  10.7 us
    all_to_all x1, waiting for transfers between devices, local(): lax.all_to_all(recon.reshape(loops, cap, width), 'cell', split_axis=0, co...  5.75 us
    all_to_all x1, starting transfers between devices, local(): lax.all_to_all(recon.reshape(loops, cap, width), 'cell', split_axis=0, co...  3.65 us
    scatter x1, other arithmetic, local(): jnp.zeros((loops * cap, width), jnp.bfloat16).at[slots].set(dequant)  2.28 us
    unnamed x8, local copies, waits for them, and re-layouts  1.6 us
  transfers between devices with their start and end apart: 2, of which 2 were waited for; matrix products, arithmetic and copies ran while one was open for 8% of the time, Pallas kernels for 0%

profile of v2, /device:TPU:0, one launch (start us, length us, event | category | flops | bytes accessed | tf_op | source)
XLA Modules:
  0.0 76.2 jit_solution(17835274254723543952)
XLA Ops:
  7.2 0.0 all-gather.2.cloned.1.call-start
  7.2 0.7 all-gather.2.cloned.1.call-update
  7.9 0.7 fusion.4
  8.6 1.2 %reduce-window.6 = s32[4,4,128]{2,1,0:T(4,128)S(1)} reduce-window(s32[4,4,128]{2,1,0:T(4,128)S(1)} %fusion.4, s32[]{:T(128)} %constant.4.clone.1), window={size=1x1x128 pad=0_0x0_0x127_0}, to_apply=%region_0.0 | reduce-window | flops 260096 | bytes 16388 | tf_op jit(solution)/shard_map/reduce-window
  9.8 0.2 slice_reduce_fusion
  10.0 0.2 reduce-window.9
  10.2 0.1 add_bitcast_fusion
  10.3 0.7 fusion.3
  11.0 0.7 compare_select_fusion
  11.7 2.3 %scatter_custom_fusion = bf16[1024,128]{1,0:T(8,128)(2,1)S(1)} fusion(s32[512]{0:T(512)S(1)} %compare_select_fusion, bf16[]{:T(256)} %constant.5.clone.1, bf16[512,128]{1,0:T(8,128)(2,1)} %param.4, f32[512]{0:T(512)} %param.5), kind=kCustom, calls=%fused_computation.4 | custom fusion | flops 196608 | bytes 395266 | tf_op jit(solution)/shard_map/scatter | solution.py:88
  14.0 10.7 %all_to_all.10 = bf16[4,256,128]{2,1,0:T(8,128)(2,1)S(1)} all-to-all(bf16[4,256,128]{2,1,0:T(8,128)(2,1)S(1)} %bitcast.22), channel_id=1, replica_groups=mesh['cell'=4,'blk'=8] {'cell'}, dimensions={0} | all-to-all | bytes 524288 | tf_op jit(solution)/shard_map/all_to_all | solution.py:89
  24.7 16.8 %all-gather.2.cloned.1.call-done.c_ref = bf16[8192,128]{1,0:T(8,128)(2,1)} async-done(((bf16[1024,128]{1,0:T(8,128)(2,1)}), bf16[8192,128]{1,0:T(8,128)(2,1)}) %all-gather.2.cloned.1.call-update) | async-done | bytes 2097168 | tf_op jit(solution)/shard_map/all_gather | solution.py:93
  41.5 0.0 copy-start
  41.5 1.6 %copy-done = bf16[8192,128]{1,0:T(8,128)(2,1)S(1)} copy-done((bf16[8192,128]{1,0:T(8,128)(2,1)S(1)}, bf16[8192,128]{1,0:T(8,128)(2,1)}, u32[]{:S(2)}) %copy-start) | copy-done | bytes 2097176
  43.1 0.0 copy-start.2
  43.1 0.0 copy-start.3
  43.1 14.7 %shard_map.59 = bf16[1024,128]{1,0:T(8,128)(2,1)} custom-call(bf16[1024,128]{1,0:T(8,128)(2,1)S(1)} %bitcast.20, bf16[8192,128]{1,0:T(8,128)(2,1)S(1)} %copy-done), custom_call_target="tpu_custom_call" | custom-call | flops 4294967296 | bytes 2621440 | tf_op jit(solution)/shard_map/pallas_call | solution.py:55
  57.8 3.6 %all-to-all-start.1 = ((bf16[4,256,128]{2,1,0:T(8,128)(2,1)}), bf16[4,256,128]{2,1,0:T(8,128)(2,1)S(1)}, u32[]{:S(2)}, u32[]{:S(2)}) async-start(bf16[4,256,128]{2,1,0:T(8,128)(2,1)} %bitcast.4), calls=%async_computation.1 | async-start | bytes 524288 | tf_op jit(solution)/shard_map/all_to_all | solution.py:95
  61.5 5.8 %all-to-all-done.1 = bf16[4,256,128]{2,1,0:T(8,128)(2,1)S(1)} async-done(((bf16[4,256,128]{2,1,0:T(8,128)(2,1)}), bf16[4,256,128]{2,1,0:T(8,128)(2,1)S(1)}, u32[]{:S(2)}, u32[]{:S(2)}) %all-to-all-start.1) | async-done | bytes 262176 | tf_op jit(solution)/shard_map/all_to_all | solution.py:95
  67.2 1.3 %gather_fusion = bf16[512,128]{1,0:T(8,128)(2,1)S(1)} fusion(bf16[1024,128]{1,0:T(8,128)(2,1)S(1)} %bitcast.21, s32[1024]{0:T(1024)S(1)} %pad_clamp_fusion), kind=kCustom, calls=%fused_computation | custom fusion | bytes 264192 | tf_op jit(solution)/shard_map/gather | solution.py:98
  68.6 0.0 copy-done.2
  68.6 0.0 copy-done.3
  68.6 0.0 copy-start.1
  68.6 0.8 %subtract_convert_fusion = bf16[512,128]{1,0:T(8,128)(2,1)} fusion(bf16[512,128]{1,0:T(8,128)(2,1)S(1)} %gather_fusion, f32[512]{0:T(512)S(1)} %copy-done.3, bf16[512,128]{1,0:T(8,128)(2,1)S(1)} %copy-done.2), kind=kLoop, calls=%fused_computation.2 | loop fusion | flops 458752 | bytes 395264 | tf_op jit(solution)/shard_map/convert_element_type | solution.py:99
  69.4 0.0 copy-done.1
  (1 shorter events, 0.0 us)
Async XLA Ops:
  7.2 34.3 %all-gather.2.cloned.1.call-start = ((), (), s32[]{:S(2)}) async-start(), calls=%async_computation.2 | async-start | bytes 2359296 | tf_op jit(solution)/shard_map/all_gather | solution.py:93
  41.5 1.6 %copy-start = (bf16[8192,128]{1,0:T(8,128)(2,1)S(1)}, bf16[8192,128]{1,0:T(8,128)(2,1)}, u32[]{:S(2)}) copy-start(bf16[8192,128]{1,0:T(8,128)(2,1)} %all-gather.2.cloned.1.call-done.c_ref) | copy-start | bytes 6291460
  43.1 25.5 %copy-start.2 = (bf16[512,128]{1,0:T(8,128)(2,1)S(1)}, bf16[512,128]{1,0:T(8,128)(2,1)}, u32[]{:S(2)}) copy-start(bf16[512,128]{1,0:T(8,128)(2,1)} %param.4) | copy-start | bytes 393220
  43.1 25.5 %copy-start.3 = (f32[512]{0:T(512)S(1)}, f32[512]{0:T(512)}, u32[]{:S(2)}) copy-start(f32[512]{0:T(512)} %param.5) | copy-start | bytes 6148
  57.8 9.4 %all-to-all-start.1 = ((bf16[4,256,128]{2,1,0:T(8,128)(2,1)}), bf16[4,256,128]{2,1,0:T(8,128)(2,1)S(1)}, u32[]{:S(2)}, u32[]{:S(2)}) async-start(bf16[4,256,128]{2,1,0:T(8,128)(2,1)} %bitcast.4), calls=%async_computation.1 | async-start | bytes 524288 | tf_op jit(solution)/shard_map/all_to_all | solution.py:95
  68.6 0.8 %copy-start.1 = (bf16[512,128]{1,0:T(8,128)(2,1)}, bf16[512,128]{1,0:T(8,128)(2,1)S(1)}, u32[]{:S(2)}) copy-start(bf16[512,128]{1,0:T(8,128)(2,1)S(1)} %gather_fusion) | copy-start | bytes 393220
Sparse Core Ops, SparseCore 0:
  9.6 31.8 all-gather.1

commit v3 on v2

--- a/solution.py
+++ b/solution.py
@@ -76,26 +76,40 @@
     )(queries, cents)
 
 
+def _shift(x, axis, n, d):
+    return lax.ppermute(x, axis, [(i, (i + d) % n) for i in range(n)])
+
+
+def _gather_partition(centroids):
+    n_blk = lax.axis_size("blk")
+    n_chip = n_blk // 2
+    pieces = [centroids]
+    for d in range(1, n_chip):
+        pairs = [(k * 2 + c, ((k + d) % n_chip) * 2 + c) for k in range(n_chip) for c in range(2)]
+        pieces.append(lax.ppermute(centroids, "blk", pairs))
+    half = jnp.concatenate(pieces, axis=0)
+    other = lax.ppermute(half, "blk", [(b, b ^ 1) for b in range(n_blk)])
+    return jnp.concatenate([half, other], axis=0)
+
+
 def local(codes, scales, coarse_ids, centroids):
     rows_dev = codes.shape[0]
     width = codes.shape[1]
     loops = lax.axis_size("cell")
     cap = 2 * rows_dev // loops
+    me = lax.axis_index("cell")
     dequant = (codes.astype(jnp.float32) * scales[:, None]).astype(jnp.bfloat16)
     onehot = (coarse_ids[:, None] == jnp.arange(loops, dtype=jnp.int32)[None, :]).astype(jnp.int32)
     ranks = jnp.sum(jnp.cumsum(onehot, axis=0) * onehot, axis=1) - 1
-    slots = coarse_ids * cap + ranks
+    slots = ((coarse_ids - me) % loops) * cap + ranks
     outgoing = jnp.zeros((loops * cap, width), jnp.bfloat16).at[slots].set(dequant)
-    arrived = lax.all_to_all(
-        outgoing.reshape(loops, cap, width), "cell", split_axis=0, concat_axis=0, tiled=True
-    )
-    queries = arrived.reshape(loops * cap, width)
-    part = lax.all_gather(centroids, "blk", axis=0, tiled=True)
-    recon = soft_reconstruct(queries, part)
-    back = lax.all_to_all(
-        recon.reshape(loops, cap, width), "cell", split_axis=0, concat_axis=0, tiled=True
-    ).reshape(loops * cap, width)
-    mine = back[slots]
+    outgoing = outgoing.reshape(loops, cap, width)
+    part = _gather_partition(centroids)
+    arrived = [outgoing[0]] + [_shift(outgoing[d], "cell", loops, d) for d in range(1, loops)]
+    queries = jnp.concatenate(arrived, axis=0)
+    recon = soft_reconstruct(queries, part).reshape(loops, cap, width)
+    back = [recon[0]] + [_shift(recon[d], "cell", loops, -d) for d in range(1, loops)]
+    mine = jnp.concatenate(back, axis=0)[slots]
     residual = (dequant.astype(jnp.float32) - mine.astype(jnp.float32)).astype(jnp.bfloat16)
     return (mine, residual)
 

time: 76.6 us -> 62.1 us (0.81)
  the two profiles are of different devices: /device:TPU:0 before, /device:TPU:8 now
where the time goes in v3:
time: 62.1 us; the launch traced here: 61.9 us
  waiting for transfers between devices  26.1 us (42%)
  Pallas kernels  14.1 us (23%)
  starting transfers between devices  12.4 us (20%)
  other arithmetic  6.66 us (11%)
  local copies, waits for them, and re-layouts  1.89 us (3%)
  between operations  0.8 us (1%)
    ppermute x3, waiting for transfers between devices, _gather_partition(): pieces.append(lax.ppermute(centroids, 'blk', pairs))  18.3 us
    pallas_call x1, Pallas kernels, soft_reconstruct(): pl.pallas_call(functools.partial(_soft_kernel, chunk=chunk, beta=1.0 / ma...  14.1 us
    ppermute x6, waiting for transfers between devices, _shift(): return lax.ppermute(x, axis, [(i, (i + d) % n) for i in range(n)])  7.75 us
    ppermute x6, starting transfers between devices, _shift(): return lax.ppermute(x, axis, [(i, (i + d) % n) for i in range(n)])  7.6 us
    ppermute x3, starting transfers between devices, _gather_partition(): pieces.append(lax.ppermute(centroids, 'blk', pairs))  4.67 us
    scatter x1, other arithmetic, local(): jnp.zeros((loops * cap, width), jnp.bfloat16).at[slots].set(dequant)  1.94 us
    another operation x2, other arithmetic  1.39 us
    gather x1, local copies, waits for them, and re-layouts, local(): mine = jnp.concatenate(back, axis=0)[slots]  1.34 us
  transfers between devices with their start and end apart: 10, of which 9 were waited for; matrix products, arithmetic and copies ran while one was open for 8% of the time, Pallas kernels for 0%

profile of v3, /device:TPU:8, one launch (start us, length us, event | category | flops | bytes accessed | tf_op | source)
XLA Modules:
  0.0 61.9 jit_solution(5864761457656735547)
XLA Ops:
  0.6 0.0 copy-start
  0.6 0.0 copy-start.3
  0.7 0.0 copy-start.2
  0.7 0.0 copy-start.4
  0.7 1.6 %collective-permute-start.3 = (bf16[1024,128]{1,0:T(8,128)(2,1)}, bf16[1024,128]{1,0:T(8,128)(2,1)S(1)}, u32[]{:S(2)}, u32[]{:S(2)}) collective-permute-start(bf16[1024,128]{1,0:T(8,128)(2,1)} %param.7), channel_id=1, source_target_pairs={{0,2},{1,3},{2,4},{3,5},{4,6},{5,7},{6,0},{7,1},{8,10},{9,11},{10,... | collective-permute-start | bytes 786440 | tf_op jit(solution)/shard_map/ppermute | solution.py:89
  2.3 1.1 %collective-permute-start.4 = (bf16[1024,128]{1,0:T(8,128)(2,1)}, bf16[1024,128]{1,0:T(8,128)(2,1)S(1)}, u32[]{:S(2)}, u32[]{:S(2)}) collective-permute-start(bf16[1024,128]{1,0:T(8,128)(2,1)} %param.7), channel_id=1, source_target_pairs={{0,4},{1,5},{2,6},{3,7},{4,0},{5,1},{6,2},{7,3},{8,12},{9,13},{10,... | collective-permute-start | bytes 786440 | tf_op jit(solution)/shard_map/ppermute | solution.py:89
  3.4 1.9 %collective-permute-start.5 = (bf16[1024,128]{1,0:T(8,128)(2,1)}, bf16[1024,128]{1,0:T(8,128)(2,1)S(1)}, u32[]{:S(2)}, u32[]{:S(2)}) collective-permute-start(bf16[1024,128]{1,0:T(8,128)(2,1)} %param.7), channel_id=1, source_target_pairs={{0,6},{1,7},{2,0},{3,1},{4,2},{5,3},{6,4},{7,5},{8,14},{9,15},{10,... | collective-permute-start | bytes 786440 | tf_op jit(solution)/shard_map/ppermute | solution.py:89
  5.3 0.7 %fusion.4 = s32[4,4,128]{2,1,0:T(4,128)S(1)} fusion(s32[4,128]{1,0:T(4,128)} %bitcast.16), kind=kLoop, calls=%fused_computation.21 | loop fusion | flops 4096 | bytes 10240 | tf_op jit(solution)/shard_map/convert_element_type | solution.py:102
  6.0 1.2 %reduce-window.6 = s32[4,4,128]{2,1,0:T(4,128)S(1)} reduce-window(s32[4,4,128]{2,1,0:T(4,128)S(1)} %fusion.4, s32[]{:T(128)} %constant.29.clone.1), window={size=1x1x128 pad=0_0x0_0x127_0}, to_apply=%region_0.0 | reduce-window | flops 260096 | bytes 16388 | tf_op jit(solution)/shard_map/reduce-window
  7.2 0.2 slice_reduce_fusion
  7.4 0.2 reduce-window.9
  7.6 0.1 add_bitcast_fusion
  7.7 0.7 %fusion.3 = s32[512]{0:T(512)S(1)} fusion(s32[1,4,4,128]{3,2,1,0:T(4,128)S(1)} %add_bitcast_fusion, s32[512]{0:T(512)} %param.6), kind=kLoop, calls=%fused_computation.16 | loop fusion | flops 5632 | bytes 12288 | tf_op jit(solution)/shard_map/reduce_sum | solution.py:103
  8.4 12.1 %collective-permute-done.3 = bf16[1024,128]{1,0:T(8,128)(2,1)S(1)} collective-permute-done((bf16[1024,128]{1,0:T(8,128)(2,1)}, bf16[1024,128]{1,0:T(8,128)(2,1)S(1)}, u32[]{:S(2)}, u32[]{:S(2)}) %collective-permute-start.3) | collective-permute-done | bytes 262176 | tf_op jit(solution)/shard_map/ppermute | solution.py:89
  20.5 4.5 %collective-permute-done.4 = bf16[1024,128]{1,0:T(8,128)(2,1)S(1)} collective-permute-done((bf16[1024,128]{1,0:T(8,128)(2,1)}, bf16[1024,128]{1,0:T(8,128)(2,1)S(1)}, u32[]{:S(2)}, u32[]{:S(2)}) %collective-permute-start.4) | collective-permute-done | bytes 262176 | tf_op jit(solution)/shard_map/ppermute | solution.py:89
  25.0 1.7 %collective-permute-done.5 = bf16[1024,128]{1,0:T(8,128)(2,1)S(1)} collective-permute-done((bf16[1024,128]{1,0:T(8,128)(2,1)}, bf16[1024,128]{1,0:T(8,128)(2,1)S(1)}, u32[]{:S(2)}, u32[]{:S(2)}) %collective-permute-start.5) | collective-permute-done | bytes 262176 | tf_op jit(solution)/shard_map/ppermute | solution.py:89
  26.7 1.0 %pad_maximum_fusion = bf16[4096,128]{1,0:T(8,128)(2,1)S(1)} fusion(bf16[1024,128]{1,0:T(8,128)(2,1)S(1)} %collective-permute-done.5, bf16[1024,128]{1,0:T(8,128)(2,1)S(1)} %collective-permute-done.4, bf16[1024,128]{1,0:T(8,128)(2,1)S(1)} %collective-permute-done.3, bf16[1024,128]{1,0:T(8,128)(2,1)} %param.7), kind=kLoop, calls=%fused_computation.2 | loop fusion | flops 4194304 | bytes 2097152 | tf_op jit(solution)/shard_map/concatenate | solution.py:90
  27.8 0.1 collective-permute-start.6
  27.8 0.0 copy-done.3
  27.9 0.0 copy-done.2
  27.9 0.0 copy-done.4
  27.9 1.9 %scatter_custom_fusion = bf16[1024,128]{1,0:T(8,128)(2,1)S(1)} fusion(s32[512]{0:T(512)S(1)} %compare_select_fusion, bf16[]{:T(256)} %constant.27.clone.1, bf16[512,128]{1,0:T(8,128)(2,1)S(1)} %copy-done.2, f32[512]{0:T(512)S(1)} %copy-done.4), kind=kCustom, calls=%fused_computation.7 | custom fusion | flops 196608 | bytes 395266 | tf_op jit(solution)/shard_map/scatter | solution.py:105
  29.9 1.5 %collective-permute-start = (bf16[256,128]{1,0:T(8,128)(2,1)S(1)}, bf16[256,128]{1,0:T(8,128)(2,1)S(1)}, u32[]{:S(2)}, u32[]{:S(2)}) collective-permute-start(bf16[256,128]{1,0:T(8,128)(2,1)S(1)} %get-tuple-element.9), channel_id=1, source_target_pairs={{0,8},{8,16},{16,24},{24,0},{1,9},{9,17},{17,25},{25,1},{2,10},{10... | collective-permute-start | bytes 196616 | tf_op jit(solution)/shard_map/ppermute | solution.py:80
  31.4 1.5 %collective-permute-start.1 = (bf16[256,128]{1,0:T(8,128)(2,1)S(1)}, bf16[256,128]{1,0:T(8,128)(2,1)S(1)}, u32[]{:S(2)}, u32[]{:S(2)}) collective-permute-start(bf16[256,128]{1,0:T(8,128)(2,1)S(1)} %get-tuple-element.8), channel_id=1, source_target_pairs={{0,16},{8,24},{16,0},{24,8},{1,17},{9,25},{17,1},{25,9},{2,18},{10... | collective-permute-start | bytes 196616 | tf_op jit(solution)/shard_map/ppermute | solution.py:80
  32.9 1.4 %collective-permute-start.2 = (bf16[256,128]{1,0:T(8,128)(2,1)S(1)}, bf16[256,128]{1,0:T(8,128)(2,1)S(1)}, u32[]{:S(2)}, u32[]{:S(2)}) collective-permute-start(bf16[256,128]{1,0:T(8,128)(2,1)S(1)} %get-tuple-element.7), channel_id=1, source_target_pairs={{0,24},{8,0},{16,8},{24,16},{1,25},{9,1},{17,9},{25,17},{2,26},{10... | collective-permute-start | bytes 196616 | tf_op jit(solution)/shard_map/ppermute | solution.py:80
  34.4 0.0 copy-done
  34.4 1.0 %collective-permute-done = bf16[256,128]{1,0:T(8,128)(2,1)S(1)} collective-permute-done((bf16[256,128]{1,0:T(8,128)(2,1)S(1)}, bf16[256,128]{1,0:T(8,128)(2,1)S(1)}, u32[]{:S(2)}, u32[]{:S(2)}) %collective-permute-start) | collective-permute-done | bytes 65568 | tf_op jit(solution)/shard_map/ppermute | solution.py:80
  35.4 1.3 %collective-permute-done.1 = bf16[256,128]{1,0:T(8,128)(2,1)S(1)} collective-permute-done((bf16[256,128]{1,0:T(8,128)(2,1)S(1)}, bf16[256,128]{1,0:T(8,128)(2,1)S(1)}, u32[]{:S(2)}, u32[]{:S(2)}) %collective-permute-start.1) | collective-permute-done | bytes 65568 | tf_op jit(solution)/shard_map/ppermute | solution.py:80
  36.7 0.5 collective-permute-done.2
  37.3 0.0 collective-permute-done.6
  37.3 0.1 constant_dynamic-update-slice_fusion.c_ref
  37.5 14.1 %shard_map.59 = bf16[1024,128]{1,0:T(8,128)(2,1)S(1)} custom-call(bf16[1024,128]{1,0:T(8,128)(2,1)S(1)} %pad_maximum_fusion.1.q_ref, bf16[8192,128]{1,0:T(8,128)(2,1)S(1)} %constant_dynamic-update-slice_fusion.c_ref), custom_call_target="tpu_custom_call" | custom-call | flops 4294967296 | bytes 2621440 | tf_op jit(solution)/shard_map/pallas_call | solution.py:55
  51.6 2.4 %collective-permute-start.7 = (bf16[256,128]{1,0:T(8,128)(2,1)S(1)}, bf16[256,128]{1,0:T(8,128)(2,1)S(1)}, u32[]{:S(2)}, u32[]{:S(2)}) collective-permute-start(bf16[256,128]{1,0:T(8,128)(2,1)S(1)} %get-tuple-element.5), channel_id=1, source_target_pairs={{0,24},{8,0},{16,8},{24,16},{1,25},{9,1},{17,9},{25,17},{2,26},{10... | collective-permute-start | bytes 196616 | tf_op jit(solution)/shard_map/ppermute | solution.py:80
  54.0 0.5 collective-permute-start.8
  54.5 0.2 collective-permute-start.9
  54.8 1.2 %collective-permute-done.7 = bf16[256,128]{1,0:T(8,128)(2,1)S(1)} collective-permute-done((bf16[256,128]{1,0:T(8,128)(2,1)S(1)}, bf16[256,128]{1,0:T(8,128)(2,1)S(1)}, u32[]{:S(2)}, u32[]{:S(2)}) %collective-permute-start.7) | collective-permute-done | bytes 65568 | tf_op jit(solution)/shard_map/ppermute | solution.py:80
  56.0 2.3 %collective-permute-done.8 = bf16[256,128]{1,0:T(8,128)(2,1)S(1)} collective-permute-done((bf16[256,128]{1,0:T(8,128)(2,1)S(1)}, bf16[256,128]{1,0:T(8,128)(2,1)S(1)}, u32[]{:S(2)}, u32[]{:S(2)}) %collective-permute-start.8) | collective-permute-done | bytes 65568 | tf_op jit(solution)/shard_map/ppermute | solution.py:80
  58.3 1.4 %collective-permute-done.9 = bf16[256,128]{1,0:T(8,128)(2,1)S(1)} collective-permute-done((bf16[256,128]{1,0:T(8,128)(2,1)S(1)}, bf16[256,128]{1,0:T(8,128)(2,1)S(1)}, u32[]{:S(2)}, u32[]{:S(2)}) %collective-permute-start.9) | collective-permute-done | bytes 65568 | tf_op jit(solution)/shard_map/ppermute | solution.py:80
  59.7 1.3 %gather_fusion = bf16[512,128]{1,0:T(8,128)(2,1)S(1)} fusion(bf16[1024,128]{1,0:T(8,128)(2,1)S(1)} %pad_maximum_fusion.2, s32[1024]{0:T(1024)S(1)} %pad_clamp_fusion), kind=kCustom, calls=%fused_computation | custom fusion | bytes 264192 | tf_op jit(solution)/shard_map/gather | solution.py:112
  61.1 0.0 copy-start.1
  61.1 0.8 %subtract_convert_fusion = bf16[512,128]{1,0:T(8,128)(2,1)} fusion(bf16[512,128]{1,0:T(8,128)(2,1)S(1)} %gather_fusion, f32[512]{0:T(512)S(1)} %copy-done.4, bf16[512,128]{1,0:T(8,128)(2,1)S(1)} %copy-done.2), kind=kLoop, calls=%fused_computation.5 | loop fusion | flops 458752 | bytes 395264 | tf_op jit(solution)/shard_map/convert_element_type | solution.py:113
  61.9 0.0 copy-done.1
  (10 shorter events, 0.2 us)
Async XLA Ops:
  0.6 33.7 %copy-start = (bf16[1024,128]{1,0:T(8,128)(2,1)S(1)}, bf16[1024,128]{1,0:T(8,128)(2,1)}, u32[]{:S(2)}) copy-start(bf16[1024,128]{1,0:T(8,128)(2,1)} %param.7) | copy-start | bytes 786436
  0.6 27.2 %copy-start.3 = (s32[512]{0:T(512)S(1)}, s32[512]{0:T(512)}, u32[]{:S(2)}) copy-start(s32[512]{0:T(512)} %param.6) | copy-start | bytes 6148
  0.7 27.2 %copy-start.2 = (bf16[512,128]{1,0:T(8,128)(2,1)S(1)}, bf16[512,128]{1,0:T(8,128)(2,1)}, u32[]{:S(2)}) copy-start(bf16[512,128]{1,0:T(8,128)(2,1)} %param.4) | copy-start | bytes 393220
  0.7 27.2 %copy-start.4 = (f32[512]{0:T(512)S(1)}, f32[512]{0:T(512)}, u32[]{:S(2)}) copy-start(f32[512]{0:T(512)} %param.5) | copy-start | bytes 6148
  0.7 19.9 %collective-permute-start.3 = (bf16[1024,128]{1,0:T(8,128)(2,1)}, bf16[1024,128]{1,0:T(8,128)(2,1)S(1)}, u32[]{:S(2)}, u32[]{:S(2)}) collective-permute-start(bf16[1024,128]{1,0:T(8,128)(2,1)} %param.7), channel_id=1, source_target_pairs={{0,2},{1,3},{2,4},{3,5},{4,6},{5,7},{6,0},{7,1},{8,10},{9,11},{10,... | collective-permute-start | bytes 786440 | tf_op jit(solution)/shard_map/ppermute | solution.py:89
  2.3 22.7 %collective-permute-start.4 = (bf16[1024,128]{1,0:T(8,128)(2,1)}, bf16[1024,128]{1,0:T(8,128)(2,1)S(1)}, u32[]{:S(2)}, u32[]{:S(2)}) collective-permute-start(bf16[1024,128]{1,0:T(8,128)(2,1)} %param.7), channel_id=1, source_target_pairs={{0,4},{1,5},{2,6},{3,7},{4,0},{5,1},{6,2},{7,3},{8,12},{9,13},{10,... | collective-permute-start | bytes 786440 | tf_op jit(solution)/shard_map/ppermute | solution.py:89
  3.4 23.3 %collective-permute-start.5 = (bf16[1024,128]{1,0:T(8,128)(2,1)}, bf16[1024,128]{1,0:T(8,128)(2,1)S(1)}, u32[]{:S(2)}, u32[]{:S(2)}) collective-permute-start(bf16[1024,128]{1,0:T(8,128)(2,1)} %param.7), channel_id=1, source_target_pairs={{0,6},{1,7},{2,0},{3,1},{4,2},{5,3},{6,4},{7,5},{8,14},{9,15},{10,... | collective-permute-start | bytes 786440 | tf_op jit(solution)/shard_map/ppermute | solution.py:89
  27.8 9.6 %collective-permute-start.6 = (bf16[4096,128]{1,0:T(8,128)(2,1)S(1)}, bf16[4096,128]{1,0:T(8,128)(2,1)S(1)}, u32[]{:S(2)}, u32[]{:S(2)}) collective-permute-start(bf16[4096,128]{1,0:T(8,128)(2,1)S(1)} %pad_maximum_fusion), channel_id=1, source_target_pairs={{0,1},{1,0},{2,3},{3,2},{4,5},{5,4},{6,7},{7,6},{8,9},{9,8},{10,11... | collective-permute-start | bytes 3145736 | tf_op jit(solution)/shard_map/ppermute | solution.py:91
  29.9 5.5 %collective-permute-start = (bf16[256,128]{1,0:T(8,128)(2,1)S(1)}, bf16[256,128]{1,0:T(8,128)(2,1)S(1)}, u32[]{:S(2)}, u32[]{:S(2)}) collective-permute-start(bf16[256,128]{1,0:T(8,128)(2,1)S(1)} %get-tuple-element.9), channel_id=1, source_target_pairs={{0,8},{8,16},{16,24},{24,0},{1,9},{9,17},{17,25},{25,1},{2,10},{10... | collective-permute-start | bytes 196616 | tf_op jit(solution)/shard_map/ppermute | solution.py:80
  31.4 5.3 %collective-permute-start.1 = (bf16[256,128]{1,0:T(8,128)(2,1)S(1)}, bf16[256,128]{1,0:T(8,128)(2,1)S(1)}, u32[]{:S(2)}, u32[]{:S(2)}) collective-permute-start(bf16[256,128]{1,0:T(8,128)(2,1)S(1)} %get-tuple-element.8), channel_id=1, source_target_pairs={{0,16},{8,24},{16,0},{24,8},{1,17},{9,25},{17,1},{25,9},{2,18},{10... | collective-permute-start | bytes 196616 | tf_op jit(solution)/shard_map/ppermute | solution.py:80
  32.9 4.3 %collective-permute-start.2 = (bf16[256,128]{1,0:T(8,128)(2,1)S(1)}, bf16[256,128]{1,0:T(8,128)(2,1)S(1)}, u32[]{:S(2)}, u32[]{:S(2)}) collective-permute-start(bf16[256,128]{1,0:T(8,128)(2,1)S(1)} %get-tuple-element.7), channel_id=1, source_target_pairs={{0,24},{8,0},{16,8},{24,16},{1,25},{9,1},{17,9},{25,17},{2,26},{10... | collective-permute-start | bytes 196616 | tf_op jit(solution)/shard_map/ppermute | solution.py:80
  51.6 4.3 %collective-permute-start.7 = (bf16[256,128]{1,0:T(8,128)(2,1)S(1)}, bf16[256,128]{1,0:T(8,128)(2,1)S(1)}, u32[]{:S(2)}, u32[]{:S(2)}) collective-permute-start(bf16[256,128]{1,0:T(8,128)(2,1)S(1)} %get-tuple-element.5), channel_id=1, source_target_pairs={{0,24},{8,0},{16,8},{24,16},{1,25},{9,1},{17,9},{25,17},{2,26},{10... | collective-permute-start | bytes 196616 | tf_op jit(solution)/shard_map/ppermute | solution.py:80
  54.0 4.3 %collective-permute-start.8 = (bf16[256,128]{1,0:T(8,128)(2,1)S(1)}, bf16[256,128]{1,0:T(8,128)(2,1)S(1)}, u32[]{:S(2)}, u32[]{:S(2)}) collective-permute-start(bf16[256,128]{1,0:T(8,128)(2,1)S(1)} %get-tuple-element.4), channel_id=1, source_target_pairs={{0,16},{8,24},{16,0},{24,8},{1,17},{9,25},{17,1},{25,9},{2,18},{10... | collective-permute-start | bytes 196616 | tf_op jit(solution)/shard_map/ppermute | solution.py:80
  54.5 5.2 %collective-permute-start.9 = (bf16[256,128]{1,0:T(8,128)(2,1)S(1)}, bf16[256,128]{1,0:T(8,128)(2,1)S(1)}, u32[]{:S(2)}, u32[]{:S(2)}) collective-permute-start(bf16[256,128]{1,0:T(8,128)(2,1)S(1)} %get-tuple-element.3), channel_id=1, source_target_pairs={{0,8},{8,16},{16,24},{24,0},{1,9},{9,17},{17,25},{25,1},{2,10},{10... | collective-permute-start | bytes 196616 | tf_op jit(solution)/shard_map/ppermute | solution.py:80
  61.1 0.8 %copy-start.1 = (bf16[512,128]{1,0:T(8,128)(2,1)}, bf16[512,128]{1,0:T(8,128)(2,1)S(1)}, u32[]{:S(2)}) copy-start(bf16[512,128]{1,0:T(8,128)(2,1)S(1)} %gather_fusion) | copy-start | bytes 393220

commit v4 on v3

--- a/solution.py
+++ b/solution.py
@@ -83,13 +83,25 @@
 def _gather_partition(centroids):
     n_blk = lax.axis_size("blk")
     n_chip = n_blk // 2
-    pieces = [centroids]
-    for d in range(1, n_chip):
-        pairs = [(k * 2 + c, ((k + d) % n_chip) * 2 + c) for k in range(n_chip) for c in range(2)]
-        pieces.append(lax.ppermute(centroids, "blk", pairs))
-    half = jnp.concatenate(pieces, axis=0)
-    other = lax.ppermute(half, "blk", [(b, b ^ 1) for b in range(n_blk)])
-    return jnp.concatenate([half, other], axis=0)
+    chip = lax.axis_index("blk") // 2
+
+    def over_chips(x, moves):
+        return lax.ppermute(x, "blk", [(k * 2 + c, j * 2 + c) for k, j in moves for c in range(2)])
+
+    if n_chip == 4:
+        up = over_chips(centroids, [(0, 1), (1, 2), (2, 3)])
+        down = over_chips(centroids, [(1, 0), (2, 1), (3, 2)])
+        two = over_chips(centroids, [(0, 2), (1, 3), (2, 0), (3, 1)])
+        relay = over_chips(two, [(2, 3), (1, 0)])
+        pieces = [centroids, jnp.where(chip == 0, relay, up), jnp.where(chip == 3, relay, down), two]
+    else:
+        pieces = [centroids] + [
+            over_chips(centroids, [(k, (k + d) % n_chip) for k in range(n_chip)])
+            for d in range(1, n_chip)
+        ]
+    swap = [(b, b ^ 1) for b in range(n_blk)]
+    swapped = [lax.ppermute(p, "blk", swap) for p in pieces]
+    return jnp.concatenate(pieces + swapped, axis=0)
 
 
 def local(codes, scales, coarse_ids, centroids):

time: 62.1 us -> 59.4 us (0.957)
  the two profiles are of different devices: /device:TPU:8 before, /device:TPU:0 now
where the time goes in v4:
time: 59.4 us; the launch traced here: 58.6 us
  starting transfers between devices  18.4 us (31%)
  waiting for transfers between devices  15.6 us (26%)
  Pallas kernels  14.1 us (24%)
  other arithmetic  6.91 us (12%)
  local copies, waits for them, and re-layouts  2.76 us (5%)
  between operations  0.87 us (1%)
    pallas_call x1, Pallas kernels, soft_reconstruct(): pl.pallas_call(functools.partial(_soft_kernel, chunk=chunk, beta=1.0 / ma...  14.1 us
    ppermute x4, starting transfers between devices, over_chips(): lax.ppermute(x, 'blk', [(k * 2 + c, j * 2 + c) for k, j in moves for c in...  10.2 us
    ppermute x4, waiting for transfers between devices, over_chips(): lax.ppermute(x, 'blk', [(k * 2 + c, j * 2 + c) for k, j in moves for c in...  9.51 us
    ppermute x6, starting transfers between devices, _shift(): return lax.ppermute(x, axis, [(i, (i + d) % n) for i in range(n)])  7.87 us
    ppermute x6, waiting for transfers between devices, _shift(): return lax.ppermute(x, axis, [(i, (i + d) % n) for i in range(n)])  4.68 us
    scatter x1, other arithmetic, local(): jnp.zeros((loops * cap, width), jnp.bfloat16).at[slots].set(dequant)  2.28 us
    another operation x2, other arithmetic  1.39 us
    ppermute x4, waiting for transfers between devices, _gather_partition(): swapped = [lax.ppermute(p, 'blk', swap) for p in pieces]  1.38 us
  transfers between devices with their start and end apart: 14, of which 8 were waited for; matrix products, arithmetic and copies ran while one was open for 13% of the time, Pallas kernels for 0%

profile of v4, /device:TPU:0, one launch (start us, length us, event | category | flops | bytes accessed | tf_op | source)
XLA Modules:
  0.0 58.6 jit_solution(14578618883048386676)
XLA Ops:
  0.6 4.1 %collective-permute-start.3 = (bf16[1024,128]{1,0:T(8,128)(2,1)}, bf16[1024,128]{1,0:T(8,128)(2,1)S(1)}, u32[]{:S(2)}, u32[]{:S(2)}) collective-permute-start(bf16[1024,128]{1,0:T(8,128)(2,1)} %param.7), channel_id=1, source_target_pairs={{0,4},{1,5},{2,6},{3,7},{4,0},{5,1},{6,2},{7,3},{8,12},{9,13},{10,... | collective-permute-start | bytes 786440 | tf_op jit(solution)/shard_map/ppermute | solution.py:89
  4.8 3.5 %collective-permute-start.5 = (bf16[1024,128]{1,0:T(8,128)(2,1)}, bf16[1024,128]{1,0:T(8,128)(2,1)S(1)}, u32[]{:S(2)}, u32[]{:S(2)}) collective-permute-start(bf16[1024,128]{1,0:T(8,128)(2,1)} %param.7), channel_id=1, source_target_pairs={{0,2},{1,3},{2,4},{3,5},{4,6},{5,7},{8,10},{9,11},{10,12},{11,13},... | collective-permute-start | bytes 786440 | tf_op jit(solution)/shard_map/ppermute | solution.py:89
  8.3 0.7 %fusion.4 = s32[4,4,128]{2,1,0:T(4,128)S(1)} fusion(s32[4,128]{1,0:T(4,128)} %bitcast.16), kind=kLoop, calls=%fused_computation.25 | loop fusion | flops 4096 | bytes 10240 | tf_op jit(solution)/shard_map/convert_element_type | solution.py:114
  8.9 1.2 %reduce-window.6 = s32[4,4,128]{2,1,0:T(4,128)S(1)} reduce-window(s32[4,4,128]{2,1,0:T(4,128)S(1)} %fusion.4, s32[]{:T(128)} %constant.43.clone.1), window={size=1x1x128 pad=0_0x0_0x127_0}, to_apply=%region_0.0 | reduce-window | flops 260096 | bytes 16388 | tf_op jit(solution)/shard_map/reduce-window
  10.1 0.2 slice_reduce_fusion
  10.4 0.2 reduce-window.9
  10.5 0.1 add_bitcast_fusion
  10.6 0.7 %fusion.3 = s32[512]{0:T(512)S(1)} fusion(s32[1,4,4,128]{3,2,1,0:T(4,128)S(1)} %add_bitcast_fusion, s32[512]{0:T(512)} %param.6), kind=kLoop, calls=%fused_computation.20 | loop fusion | flops 5632 | bytes 12288 | tf_op jit(solution)/shard_map/reduce_sum | solution.py:115
  11.3 0.7 %compare_select_fusion = s32[512]{0:T(512)S(1)} fusion(s32[512]{0:T(512)S(1)} %fusion.3, s32[512]{0:T(512)} %param.6, s32[]{:T(128)S(6)} %axis_index.23), kind=kLoop, calls=%fused_computation.26 | loop fusion | flops 9216 | bytes 6148 | tf_op jit(solution)/shard_map/select_n | solution.py:117
  12.0 2.3 %scatter_custom_fusion = bf16[1024,128]{1,0:T(8,128)(2,1)S(1)} fusion(s32[512]{0:T(512)S(1)} %compare_select_fusion, bf16[]{:T(256)} %constant.41.clone.1, bf16[512,128]{1,0:T(8,128)(2,1)} %param.4, f32[512]{0:T(512)} %param.5), kind=kCustom, calls=%fused_computation.8 | custom fusion | flops 196608 | bytes 395266 | tf_op jit(solution)/shard_map/scatter | solution.py:117
  14.3 2.6 %collective-permute-done.3 = bf16[1024,128]{1,0:T(8,128)(2,1)S(1)} collective-permute-done((bf16[1024,128]{1,0:T(8,128)(2,1)}, bf16[1024,128]{1,0:T(8,128)(2,1)S(1)}, u32[]{:S(2)}, u32[]{:S(2)}) %collective-permute-start.3) | collective-permute-done | bytes 262176 | tf_op jit(solution)/shard_map/ppermute | solution.py:89
  16.9 1.3 %collective-permute-start.4 = (bf16[1024,128]{1,0:T(8,128)(2,1)S(1)}, bf16[1024,128]{1,0:T(8,128)(2,1)S(1)}, u32[]{:S(2)}, u32[]{:S(2)}) collective-permute-start(bf16[1024,128]{1,0:T(8,128)(2,1)S(1)} %collective-permute-done.3), channel_id=1, source_target_pairs={{4,6},{5,7},{2,0},{3,1},{12,14},{13,15},{10,8},{11,9},{20,22},{21,... | collective-permute-start | bytes 786440 | tf_op jit(solution)/shard_map/ppermute | solution.py:89
  18.2 1.6 %collective-permute-start = (bf16[256,128]{1,0:T(8,128)(2,1)S(1)}, bf16[256,128]{1,0:T(8,128)(2,1)S(1)}, u32[]{:S(2)}, u32[]{:S(2)}) collective-permute-start(bf16[256,128]{1,0:T(8,128)(2,1)S(1)} %get-tuple-element.13), channel_id=1, source_target_pairs={{0,8},{8,16},{16,24},{24,0},{1,9},{9,17},{17,25},{25,1},{2,10},{10... | collective-permute-start | bytes 196616 | tf_op jit(solution)/shard_map/ppermute | solution.py:80
  19.8 1.5 %collective-permute-start.1 = (bf16[256,128]{1,0:T(8,128)(2,1)S(1)}, bf16[256,128]{1,0:T(8,128)(2,1)S(1)}, u32[]{:S(2)}, u32[]{:S(2)}) collective-permute-start(bf16[256,128]{1,0:T(8,128)(2,1)S(1)} %get-tuple-element.12), channel_id=1, source_target_pairs={{0,16},{8,24},{16,0},{24,8},{1,17},{9,25},{17,1},{25,9},{2,18},{10... | collective-permute-start | bytes 196616 | tf_op jit(solution)/shard_map/ppermute | solution.py:80
  21.3 1.4 %collective-permute-start.2 = (bf16[256,128]{1,0:T(8,128)(2,1)S(1)}, bf16[256,128]{1,0:T(8,128)(2,1)S(1)}, u32[]{:S(2)}, u32[]{:S(2)}) collective-permute-start(bf16[256,128]{1,0:T(8,128)(2,1)S(1)} %get-tuple-element.11), channel_id=1, source_target_pairs={{0,24},{8,0},{16,8},{24,16},{1,25},{9,1},{17,9},{25,17},{2,26},{10... | collective-permute-start | bytes 196616 | tf_op jit(solution)/shard_map/ppermute | solution.py:80
  22.8 1.0 %constant_dynamic-update-slice_fusion.7 = bf16[8192,128]{1,0:T(8,128)(2,1)S(1)} fusion(bf16[1024,128]{1,0:T(8,128)(2,1)} %param.7), kind=kLoop, calls=%fused_computation.17 | loop fusion | bytes 524288
  23.7 0.0 collective-permute-done
  23.7 1.3 %collective-permute-start.6 = (bf16[1024,128]{1,0:T(8,128)(2,1)}, bf16[1024,128]{1,0:T(8,128)(2,1)S(1)}, u32[]{:S(2)}, u32[]{:S(2)}) collective-permute-start(bf16[1024,128]{1,0:T(8,128)(2,1)} %param.7), channel_id=1, source_target_pairs={{2,0},{3,1},{4,2},{5,3},{6,4},{7,5},{10,8},{11,9},{12,10},{13,11},... | collective-permute-start | bytes 786440 | tf_op jit(solution)/shard_map/ppermute | solution.py:89
  25.0 0.0 collective-permute-done.1
  25.0 0.1 collective-permute-start.7
  25.1 0.5 collective-permute-done.2
  25.6 0.1 collective-permute-start.10
  25.7 0.0 collective-permute-done.5
  25.7 0.5 collective-permute-done.4
  26.2 0.1 constant_dynamic-update-slice_fusion.6
  26.4 0.1 collective-permute-start.8
  26.5 6.4 %collective-permute-done.6 = bf16[1024,128]{1,0:T(8,128)(2,1)S(1)} collective-permute-done((bf16[1024,128]{1,0:T(8,128)(2,1)}, bf16[1024,128]{1,0:T(8,128)(2,1)S(1)}, u32[]{:S(2)}, u32[]{:S(2)}) %collective-permute-start.6) | collective-permute-done | bytes 262176 | tf_op jit(solution)/shard_map/ppermute | solution.py:89
  32.9 0.1 constant_dynamic-update-slice_fusion.5
  33.0 0.1 collective-permute-start.9
  33.1 0.0 collective-permute-done.7
  33.2 0.0 collective-permute-done.8
  33.2 1.4 %collective-permute-done.9 = bf16[1024,128]{1,0:T(8,128)(2,1)S(1)} collective-permute-done((bf16[1024,128]{1,0:T(8,128)(2,1)S(1)}, bf16[1024,128]{1,0:T(8,128)(2,1)S(1)}, u32[]{:S(2)}, u32[]{:S(2)}) %collective-permute-start.9) | collective-permute-done | bytes 262176 | tf_op jit(solution)/shard_map/ppermute | solution.py:103
  34.6 0.0 collective-permute-done.10
  34.7 14.1 %shard_map.59 = bf16[1024,128]{1,0:T(8,128)(2,1)S(1)} custom-call(bf16[1024,128]{1,0:T(8,128)(2,1)S(1)} %pad_maximum_fusion.q_ref, bf16[8192,128]{1,0:T(8,128)(2,1)S(1)} %constant_dynamic-update-slice_fusion.c_ref), custom_call_target="tpu_custom_call" | custom-call | flops 4294967296 | bytes 2621440 | tf_op jit(solution)/shard_map/pallas_call | solution.py:55
  48.8 0.0 copy-start.1
  48.8 0.0 copy-start.2
  48.9 1.4 %collective-permute-start.11 = (bf16[256,128]{1,0:T(8,128)(2,1)S(1)}, bf16[256,128]{1,0:T(8,128)(2,1)S(1)}, u32[]{:S(2)}, u32[]{:S(2)}) collective-permute-start(bf16[256,128]{1,0:T(8,128)(2,1)S(1)} %get-tuple-element.9), channel_id=1, source_target_pairs={{0,24},{8,0},{16,8},{24,16},{1,25},{9,1},{17,9},{25,17},{2,26},{10... | collective-permute-start | bytes 196616 | tf_op jit(solution)/shard_map/ppermute | solution.py:80
  50.2 1.0 %collective-permute-start.12 = (bf16[256,128]{1,0:T(8,128)(2,1)S(1)}, bf16[256,128]{1,0:T(8,128)(2,1)S(1)}, u32[]{:S(2)}, u32[]{:S(2)}) collective-permute-start(bf16[256,128]{1,0:T(8,128)(2,1)S(1)} %get-tuple-element.8), channel_id=1, source_target_pairs={{0,16},{8,24},{16,0},{24,8},{1,17},{9,25},{17,1},{25,9},{2,18},{10... | collective-permute-start | bytes 196616 | tf_op jit(solution)/shard_map/ppermute | solution.py:80
  51.2 0.9 %collective-permute-start.13 = (bf16[256,128]{1,0:T(8,128)(2,1)S(1)}, bf16[256,128]{1,0:T(8,128)(2,1)S(1)}, u32[]{:S(2)}, u32[]{:S(2)}) collective-permute-start(bf16[256,128]{1,0:T(8,128)(2,1)S(1)} %get-tuple-element.7), channel_id=1, source_target_pairs={{0,8},{8,16},{16,24},{24,0},{1,9},{9,17},{17,25},{25,1},{2,10},{10... | collective-permute-start | bytes 196616 | tf_op jit(solution)/shard_map/ppermute | solution.py:80
  52.2 1.0 %collective-permute-done.11 = bf16[256,128]{1,0:T(8,128)(2,1)S(1)} collective-permute-done((bf16[256,128]{1,0:T(8,128)(2,1)S(1)}, bf16[256,128]{1,0:T(8,128)(2,1)S(1)}, u32[]{:S(2)}, u32[]{:S(2)}) %collective-permute-start.11) | collective-permute-done | bytes 65568 | tf_op jit(solution)/shard_map/ppermute | solution.py:80
  53.2 2.0 %collective-permute-done.12 = bf16[256,128]{1,0:T(8,128)(2,1)S(1)} collective-permute-done((bf16[256,128]{1,0:T(8,128)(2,1)S(1)}, bf16[256,128]{1,0:T(8,128)(2,1)S(1)}, u32[]{:S(2)}, u32[]{:S(2)}) %collective-permute-start.12) | collective-permute-done | bytes 65568 | tf_op jit(solution)/shard_map/ppermute | solution.py:80
  55.2 1.2 %collective-permute-done.13 = bf16[256,128]{1,0:T(8,128)(2,1)S(1)} collective-permute-done((bf16[256,128]{1,0:T(8,128)(2,1)S(1)}, bf16[256,128]{1,0:T(8,128)(2,1)S(1)}, u32[]{:S(2)}, u32[]{:S(2)}) %collective-permute-start.13) | collective-permute-done | bytes 65568 | tf_op jit(solution)/shard_map/ppermute | solution.py:80
  56.4 1.3 %gather_fusion = bf16[512,128]{1,0:T(8,128)(2,1)S(1)} fusion(bf16[1024,128]{1,0:T(8,128)(2,1)S(1)} %pad_maximum_fusion.1, s32[1024]{0:T(1024)S(1)} %pad_clamp_fusion), kind=kCustom, calls=%fused_computation | custom fusion | bytes 264192 | tf_op jit(solution)/shard_map/gather | solution.py:124
  57.8 0.0 copy-done.1
  57.8 0.0 copy-done.2
  57.8 0.0 copy-start
  57.8 0.8 %subtract_convert_fusion = bf16[512,128]{1,0:T(8,128)(2,1)} fusion(bf16[512,128]{1,0:T(8,128)(2,1)S(1)} %gather_fusion, f32[512]{0:T(512)S(1)} %copy-done.2, bf16[512,128]{1,0:T(8,128)(2,1)S(1)} %copy-done.1), kind=kLoop, calls=%fused_computation.4 | loop fusion | flops 458752 | bytes 395264 | tf_op jit(solution)/shard_map/convert_element_type | solution.py:125
  58.6 0.0 copy-done
  (10 shorter events, 0.3 us)
Async XLA Ops:
  0.6 16.3 %collective-permute-start.3 = (bf16[1024,128]{1,0:T(8,128)(2,1)}, bf16[1024,128]{1,0:T(8,128)(2,1)S(1)}, u32[]{:S(2)}, u32[]{:S(2)}) collective-permute-start(bf16[1024,128]{1,0:T(8,128)(2,1)} %param.7), channel_id=1, source_target_pairs={{0,4},{1,5},{2,6},{3,7},{4,0},{5,1},{6,2},{7,3},{8,12},{9,13},{10,... | collective-permute-start | bytes 786440 | tf_op jit(solution)/shard_map/ppermute | solution.py:89
  4.8 21.0 %collective-permute-start.5 = (bf16[1024,128]{1,0:T(8,128)(2,1)}, bf16[1024,128]{1,0:T(8,128)(2,1)S(1)}, u32[]{:S(2)}, u32[]{:S(2)}) collective-permute-start(bf16[1024,128]{1,0:T(8,128)(2,1)} %param.7), channel_id=1, source_target_pairs={{0,2},{1,3},{2,4},{3,5},{4,6},{5,7},{8,10},{9,11},{10,12},{11,13},... | collective-permute-start | bytes 786440 | tf_op jit(solution)/shard_map/ppermute | solution.py:89
  16.9 9.4 %collective-permute-start.4 = (bf16[1024,128]{1,0:T(8,128)(2,1)S(1)}, bf16[1024,128]{1,0:T(8,128)(2,1)S(1)}, u32[]{:S(2)}, u32[]{:S(2)}) collective-permute-start(bf16[1024,128]{1,0:T(8,128)(2,1)S(1)} %collective-permute-done.3), channel_id=1, source_target_pairs={{4,6},{5,7},{2,0},{3,1},{12,14},{13,15},{10,8},{11,9},{20,22},{21,... | collective-permute-start | bytes 786440 | tf_op jit(solution)/shard_map/ppermute | solution.py:89
  18.2 5.5 %collective-permute-start = (bf16[256,128]{1,0:T(8,128)(2,1)S(1)}, bf16[256,128]{1,0:T(8,128)(2,1)S(1)}, u32[]{:S(2)}, u32[]{:S(2)}) collective-permute-start(bf16[256,128]{1,0:T(8,128)(2,1)S(1)} %get-tuple-element.13), channel_id=1, source_target_pairs={{0,8},{8,16},{16,24},{24,0},{1,9},{9,17},{17,25},{25,1},{2,10},{10... | collective-permute-start | bytes 196616 | tf_op jit(solution)/shard_map/ppermute | solution.py:80
  19.8 5.2 %collective-permute-start.1 = (bf16[256,128]{1,0:T(8,128)(2,1)S(1)}, bf16[256,128]{1,0:T(8,128)(2,1)S(1)}, u32[]{:S(2)}, u32[]{:S(2)}) collective-permute-start(bf16[256,128]{1,0:T(8,128)(2,1)S(1)} %get-tuple-element.12), channel_id=1, source_target_pairs={{0,16},{8,24},{16,0},{24,8},{1,17},{9,25},{17,1},{25,9},{2,18},{10... | collective-permute-start | bytes 196616 | tf_op jit(solution)/shard_map/ppermute | solution.py:80
  21.3 4.3 %collective-permute-start.2 = (bf16[256,128]{1,0:T(8,128)(2,1)S(1)}, bf16[256,128]{1,0:T(8,128)(2,1)S(1)}, u32[]{:S(2)}, u32[]{:S(2)}) collective-permute-start(bf16[256,128]{1,0:T(8,128)(2,1)S(1)} %get-tuple-element.11), channel_id=1, source_target_pairs={{0,24},{8,0},{16,8},{24,16},{1,25},{9,1},{17,9},{25,17},{2,26},{10... | collective-permute-start | bytes 196616 | tf_op jit(solution)/shard_map/ppermute | solution.py:80
  23.7 9.1 %collective-permute-start.6 = (bf16[1024,128]{1,0:T(8,128)(2,1)}, bf16[1024,128]{1,0:T(8,128)(2,1)S(1)}, u32[]{:S(2)}, u32[]{:S(2)}) collective-permute-start(bf16[1024,128]{1,0:T(8,128)(2,1)} %param.7), channel_id=1, source_target_pairs={{2,0},{3,1},{4,2},{5,3},{6,4},{7,5},{10,8},{11,9},{12,10},{13,11},... | collective-permute-start | bytes 786440 | tf_op jit(solution)/shard_map/ppermute | solution.py:89
  25.0 8.1 %collective-permute-start.7 = (bf16[1024,128]{1,0:T(8,128)(2,1)}, bf16[1024,128]{1,0:T(8,128)(2,1)S(1)}, u32[]{:S(2)}, u32[]{:S(2)}) collective-permute-start(bf16[1024,128]{1,0:T(8,128)(2,1)} %param.7), channel_id=1, source_target_pairs={{0,1},{1,0},{2,3},{3,2},{4,5},{5,4},{6,7},{7,6},{8,9},{9,8},{10,11... | collective-permute-start | bytes 786440 | tf_op jit(solution)/shard_map/ppermute | solution.py:103
  25.6 9.0 %collective-permute-start.10 = (bf16[1024,128]{1,0:T(8,128)(2,1)S(1)}, bf16[1024,128]{1,0:T(8,128)(2,1)S(1)}, u32[]{:S(2)}, u32[]{:S(2)}) collective-permute-start(bf16[1024,128]{1,0:T(8,128)(2,1)S(1)} %collective-permute-done.3), channel_id=1, source_target_pairs={{0,1},{1,0},{2,3},{3,2},{4,5},{5,4},{6,7},{7,6},{8,9},{9,8},{10,11... | collective-permute-start | bytes 786440 | tf_op jit(solution)/shard_map/ppermute | solution.py:103
  26.4 6.8 %collective-permute-start.8 = (bf16[1024,128]{1,0:T(8,128)(2,1)S(1)}, bf16[1024,128]{1,0:T(8,128)(2,1)S(1)}, u32[]{:S(2)}, u32[]{:S(2)}) collective-permute-start(bf16[1024,128]{1,0:T(8,128)(2,1)S(1)} %get-tuple-element.5), channel_id=1, source_target_pairs={{0,1},{1,0},{2,3},{3,2},{4,5},{5,4},{6,7},{7,6},{8,9},{9,8},{10,11... | collective-permute-start | bytes 786440 | tf_op jit(solution)/shard_map/ppermute | solution.py:103
  33.0 1.6 %collective-permute-start.9 = (bf16[1024,128]{1,0:T(8,128)(2,1)S(1)}, bf16[1024,128]{1,0:T(8,128)(2,1)S(1)}, u32[]{:S(2)}, u32[]{:S(2)}) collective-permute-start(bf16[1024,128]{1,0:T(8,128)(2,1)S(1)} %get-tuple-element.3), channel_id=1, source_target_pairs={{0,1},{1,0},{2,3},{3,2},{4,5},{5,4},{6,7},{7,6},{8,9},{9,8},{10,11... | collective-permute-start | bytes 786440 | tf_op jit(solution)/shard_map/ppermute | solution.py:103
  48.8 9.0 %copy-start.1 = (bf16[512,128]{1,0:T(8,128)(2,1)S(1)}, bf16[512,128]{1,0:T(8,128)(2,1)}, u32[]{:S(2)}) copy-start(bf16[512,128]{1,0:T(8,128)(2,1)} %param.4) | copy-start | bytes 393220
  48.8 9.0 %copy-start.2 = (f32[512]{0:T(512)S(1)}, f32[512]{0:T(512)}, u32[]{:S(2)}) copy-start(f32[512]{0:T(512)} %param.5) | copy-start | bytes 6148
  48.9 4.3 %collective-permute-start.11 = (bf16[256,128]{1,0:T(8,128)(2,1)S(1)}, bf16[256,128]{1,0:T(8,128)(2,1)S(1)}, u32[]{:S(2)}, u32[]{:S(2)}) collective-permute-start(bf16[256,128]{1,0:T(8,128)(2,1)S(1)} %get-tuple-element.9), channel_id=1, source_target_pairs={{0,24},{8,0},{16,8},{24,16},{1,25},{9,1},{17,9},{25,17},{2,26},{10... | collective-permute-start | bytes 196616 | tf_op jit(solution)/shard_map/ppermute | solution.py:80
  50.2 5.0 %collective-permute-start.12 = (bf16[256,128]{1,0:T(8,128)(2,1)S(1)}, bf16[256,128]{1,0:T(8,128)(2,1)S(1)}, u32[]{:S(2)}, u32[]{:S(2)}) collective-permute-start(bf16[256,128]{1,0:T(8,128)(2,1)S(1)} %get-tuple-element.8), channel_id=1, source_target_pairs={{0,16},{8,24},{16,0},{24,8},{1,17},{9,25},{17,1},{25,9},{2,18},{10... | collective-permute-start | bytes 196616 | tf_op jit(solution)/shard_map/ppermute | solution.py:80
  51.2 5.2 %collective-permute-start.13 = (bf16[256,128]{1,0:T(8,128)(2,1)S(1)}, bf16[256,128]{1,0:T(8,128)(2,1)S(1)}, u32[]{:S(2)}, u32[]{:S(2)}) collective-permute-start(bf16[256,128]{1,0:T(8,128)(2,1)S(1)} %get-tuple-element.7), channel_id=1, source_target_pairs={{0,8},{8,16},{16,24},{24,0},{1,9},{9,17},{17,25},{25,1},{2,10},{10... | collective-permute-start | bytes 196616 | tf_op jit(solution)/shard_map/ppermute | solution.py:80
  57.8 0.8 %copy-start = (bf16[512,128]{1,0:T(8,128)(2,1)}, bf16[512,128]{1,0:T(8,128)(2,1)S(1)}, u32[]{:S(2)}) copy-start(bf16[512,128]{1,0:T(8,128)(2,1)S(1)} %gather_fusion) | copy-start | bytes 393220

commit v5 on v4

--- a/solution.py
+++ b/solution.py
@@ -9,7 +9,11 @@
 from jax.sharding import PartitionSpec as P
 
 
-def _soft_kernel(q_ref, c_ref, o_ref, m_sc, l_sc, acc_sc, s_sc, *, chunk, beta):
+def _soft_kernel(*refs, chunk, beta, merge):
+    if merge:
+        q_ref, c_ref, pm_ref, pl_ref, pacc_ref, o_ref, m_sc, l_sc, acc_sc, s_sc = refs
+    else:
+        q_ref, c_ref, om_ref, ol_ref, oacc_ref, m_sc, l_sc, acc_sc, s_sc = refs
     n_chunks = c_ref.shape[0] // chunk
     lanes = m_sc.shape[1]
     q = q_ref[...]
@@ -28,6 +32,8 @@
         m_sc[...] = m
 
     top = jnp.max(m_sc[...], axis=1, keepdims=True)
+    if merge:
+        top = jnp.maximum(top, pm_ref[...])
     l_sc[...] = jnp.zeros(l_sc.shape, jnp.float32)
     acc_sc[...] = jnp.zeros(acc_sc.shape, jnp.float32)
 
@@ -43,24 +49,45 @@
         acc_sc[...] += jnp.dot(w, c_ref[cols, :], preferred_element_type=jnp.float32)
 
     total = jnp.sum(l_sc[...], axis=1, keepdims=True)
-    o_ref[...] = (acc_sc[...] / total).astype(o_ref.dtype)
+    if merge:
+        scale = jnp.exp(pm_ref[...] - top)
+        total = total + pl_ref[...] * scale
+        numer = acc_sc[...] + pacc_ref[...] * scale
+        o_ref[...] = (numer / total).astype(o_ref.dtype)
+    else:
+        om_ref[...] = top
+        ol_ref[...] = total
+        oacc_ref[...] = acc_sc[...]
 
 
-def soft_reconstruct(queries, cents):
+def soft_part(queries, cents, prior=None):
     slots, width = queries.shape
     n_cent = cents.shape[0]
-    chunk = min(2048, n_cent)
-    tq = min(512, slots, (16 << 20) // (4 * n_cent))
-    vmem = 4 * tq * n_cent + 2 * 2 * n_cent * width + 8 * tq * width * 4 + (8 << 20)
+    chunk = min(4096, n_cent)
+    tq = min(1024, slots, (32 << 20) // (4 * n_cent))
+    vmem = 4 * tq * n_cent + 2 * 2 * n_cent * width + 16 * tq * width * 4 + (8 << 20)
+    rows = pl.BlockSpec((tq, width), lambda i: (i, 0))
+    col = pl.BlockSpec((tq, 1), lambda i: (i, 0))
+    in_specs = [rows, pl.BlockSpec((n_cent, width), lambda i: (0, 0))]
+    stats = [
+        jax.ShapeDtypeStruct((slots, 1), jnp.float32),
+        jax.ShapeDtypeStruct((slots, 1), jnp.float32),
+        jax.ShapeDtypeStruct((slots, width), jnp.float32),
+    ]
+    if prior is None:
+        out_shape, out_specs, args = stats, [col, col, rows], (queries, cents)
+    else:
+        in_specs += [col, col, rows]
+        out_shape = jax.ShapeDtypeStruct((slots, width), jnp.bfloat16)
+        out_specs, args = rows, (queries, cents) + tuple(prior)
     return pl.pallas_call(
-        functools.partial(_soft_kernel, chunk=chunk, beta=1.0 / math.sqrt(width)),
-        out_shape=jax.ShapeDtypeStruct((slots, width), jnp.bfloat16),
+        functools.partial(
+            _soft_kernel, chunk=chunk, beta=1.0 / math.sqrt(width), merge=prior is not None
+        ),
+        out_shape=out_shape,
         grid=(slots // tq,),
-        in_specs=[
-            pl.BlockSpec((tq, width), lambda i: (i, 0)),
-            pl.BlockSpec((n_cent, width), lambda i: (0, 0)),
-        ],
-        out_specs=pl.BlockSpec((tq, width), lambda i: (i, 0)),
+        in_specs=in_specs,
+        out_specs=out_specs,
         scratch_shapes=[
             pltpu.VMEM((tq, 128), jnp.float32),
             pltpu.VMEM((tq, 128), jnp.float32),
@@ -73,7 +100,7 @@
             transcendentals=slots * n_cent,
             bytes_accessed=2 * (2 * slots * width + n_cent * width),
         ),
-    )(queries, cents)
+    )(*args)
 
 
 def _shift(x, axis, n, d):
@@ -93,7 +120,7 @@
         down = over_chips(centroids, [(1, 0), (2, 1), (3, 2)])
         two = over_chips(centroids, [(0, 2), (1, 3), (2, 0), (3, 1)])
         relay = over_chips(two, [(2, 3), (1, 0)])
-        pieces = [centroids, jnp.where(chip == 0, relay, up), jnp.where(chip == 3, relay, down), two]
+        pieces = [centroids, two, jnp.where(chip == 0, relay, up), jnp.where(chip == 3, relay, down)]
     else:
         pieces = [centroids] + [
             over_chips(centroids, [(k, (k + d) % n_chip) for k in range(n_chip)])
@@ -101,10 +128,13 @@
         ]
     swap = [(b, b ^ 1) for b in range(n_blk)]
     swapped = [lax.ppermute(p, "blk", swap) for p in pieces]
-    return jnp.concatenate(pieces + swapped, axis=0)
+    k = len(pieces) // 2
+    early = jnp.concatenate(pieces[:k] + swapped[:k], axis=0)
+    late = jnp.concatenate(pieces[k:] + swapped[k:], axis=0)
+    return early, late
 
 
-def local(codes, scales, coarse_ids, centroids):
+def _local(codes, scales, coarse_ids, centroids):
     rows_dev = codes.shape[0]
     width = codes.shape[1]
     loops = lax.axis_size("cell")
@@ -116,10 +146,11 @@
     slots = ((coarse_ids - me) % loops) * cap + ranks
     outgoing = jnp.zeros((loops * cap, width), jnp.bfloat16).at[slots].set(dequant)
     outgoing = outgoing.reshape(loops, cap, width)
-    part = _gather_partition(centroids)
+    early, late = _gather_partition(centroids)
     arrived = [outgoing[0]] + [_shift(outgoing[d], "cell", loops, d) for d in range(1, loops)]
     queries = jnp.concatenate(arrived, axis=0)
-    recon = soft_reconstruct(queries, part).reshape(loops, cap, width)
+    prior = soft_part(queries, early)
+    recon = soft_part(queries, late, prior).reshape(loops, cap, width)
     back = [recon[0]] + [_shift(recon[d], "cell", loops, -d) for d in range(1, loops)]
     mine = jnp.concatenate(back, axis=0)[slots]
     residual = (dequant.astype(jnp.float32) - mine.astype(jnp.float32)).astype(jnp.bfloat16)
@@ -130,4 +161,4 @@
     rows = P(("cell", "blk"), None)
     in_specs = (rows, P(("cell", "blk")), P(("cell", "blk")), rows)
     out_specs = (rows, rows)
-    return jax.shard_map(local, mesh=mesh, in_specs=in_specs, out_specs=out_specs, check_vma=False)
+    return jax.shard_map(_local, mesh=mesh, in_specs=in_specs, out_specs=out_specs, check_vma=False)

time: 59.4 us -> 62.1 us (1.045)
  Pallas kernels: 14.1 us -> 20.4 us
  waiting for transfers between devices: 15.6 us -> 11.1 us
  starting transfers between devices: 18.4 us -> 20.9 us
  local copies, waits for them, and re-layouts: 2.76 us -> 1.62 us
    ppermute x4, waiting for transfers between devices: 9.51 us -> 2.17 us  [over_chips(): lax.ppermute(x, 'blk', [(k * 2 + c, j * 2 + c) for k, j in moves for c in...]
    pallas_call x1 -> x2, Pallas kernels: 14.1 us -> 20.4 us  [soft_part(): pl.pallas_call(functools.partial(_soft_kernel, chunk=chunk, beta=1.0 / ma...]
    ppermute x6, waiting for transfers between devices: 4.68 us -> 8.15 us  [_shift(): return lax.ppermute(x, axis, [(i, (i + d) % n) for i in range(n)])]
    ppermute x6, starting transfers between devices: 7.87 us -> 10 us  [_shift(): return lax.ppermute(x, axis, [(i, (i + d) % n) for i in range(n)])]
    unnamed x11 -> x8, local copies, waits for them, and re-layouts: 1.13 us -> 0.02 us
  transfers between devices with their start and end apart: 14 -> 14, of which waited for: 8 -> 6; matrix products, arithmetic and copies ran while one was open for 13% -> 10% of each run, Pallas kernels for 0% -> 20%
where the time goes in v5:
time: 62.1 us; the launch traced here: 61.7 us
  starting transfers between devices  20.9 us (34%)
  Pallas kernels  20.4 us (33%)
  waiting for transfers between devices  11.1 us (18%)
  other arithmetic  6.86 us (11%)
  local copies, waits for them, and re-layouts  1.62 us (3%)
  between operations  0.83 us (1%)
    pallas_call x2, Pallas kernels, soft_part(): pl.pallas_call(functools.partial(_soft_kernel, chunk=chunk, beta=1.0 / ma...  20.4 us
    ppermute x4, starting transfers between devices, over_chips(): lax.ppermute(x, 'blk', [(k * 2 + c, j * 2 + c) for k, j in moves for c in...  10.2 us
    ppermute x6, starting transfers between devices, _shift(): return lax.ppermute(x, axis, [(i, (i + d) % n) for i in range(n)])  10 us
    ppermute x6, waiting for transfers between devices, _shift(): return lax.ppermute(x, axis, [(i, (i + d) % n) for i in range(n)])  8.15 us
    scatter x1, other arithmetic, _local(): jnp.zeros((loops * cap, width), jnp.bfloat16).at[slots].set(dequant)  2.28 us
    ppermute x4, waiting for transfers between devices, over_chips(): lax.ppermute(x, 'blk', [(k * 2 + c, j * 2 + c) for k, j in moves for c in...  2.17 us
    another operation x2, other arithmetic  1.39 us
    gather x1, local copies, waits for them, and re-layouts, _local(): mine = jnp.concatenate(back, axis=0)[slots]  1.34 us
  transfers between devices with their start and end apart: 14, of which 6 were waited for; matrix products, arithmetic and copies ran while one was open for 10% of the time, Pallas kernels for 20%

profile of v5, /device:TPU:0, one launch (start us, length us, event | category | flops | bytes accessed | tf_op | source)
XLA Modules:
  0.0 61.7 jit_solution(11609666569373015002)
XLA Ops:
  0.6 0.0 copy-start.2
  0.6 4.1 %collective-permute-start.3 = (bf16[1024,128]{1,0:T(8,128)(2,1)}, bf16[1024,128]{1,0:T(8,128)(2,1)S(1)}, u32[]{:S(2)}, u32[]{:S(2)}) collective-permute-start(bf16[1024,128]{1,0:T(8,128)(2,1)} %param.7), channel_id=1, source_target_pairs={{0,4},{1,5},{2,6},{3,7},{4,0},{5,1},{6,2},{7,3},{8,12},{9,13},{10,... | collective-permute-start | bytes 786440 | tf_op jit(solution)/shard_map/ppermute | solution.py:116
  4.8 3.5 %collective-permute-start.5 = (bf16[1024,128]{1,0:T(8,128)(2,1)}, bf16[1024,128]{1,0:T(8,128)(2,1)S(1)}, u32[]{:S(2)}, u32[]{:S(2)}) collective-permute-start(bf16[1024,128]{1,0:T(8,128)(2,1)} %param.7), channel_id=1, source_target_pairs={{0,2},{1,3},{2,4},{3,5},{4,6},{5,7},{8,10},{9,11},{10,12},{11,13},... | collective-permute-start | bytes 786440 | tf_op jit(solution)/shard_map/ppermute | solution.py:116
  8.3 1.3 %collective-permute-start.6 = (bf16[1024,128]{1,0:T(8,128)(2,1)}, bf16[1024,128]{1,0:T(8,128)(2,1)S(1)}, u32[]{:S(2)}, u32[]{:S(2)}) collective-permute-start(bf16[1024,128]{1,0:T(8,128)(2,1)} %param.7), channel_id=1, source_target_pairs={{2,0},{3,1},{4,2},{5,3},{6,4},{7,5},{10,8},{11,9},{12,10},{13,11},... | collective-permute-start | bytes 786440 | tf_op jit(solution)/shard_map/ppermute | solution.py:116
  9.6 0.7 %fusion.4 = s32[4,4,128]{2,1,0:T(4,128)S(1)} fusion(s32[4,128]{1,0:T(4,128)} %bitcast.16), kind=kLoop, calls=%fused_computation.19 | loop fusion | flops 4096 | bytes 10240 | tf_op jit(solution)/shard_map/convert_element_type | solution.py:144
  10.2 1.2 %reduce-window.6 = s32[4,4,128]{2,1,0:T(4,128)S(1)} reduce-window(s32[4,4,128]{2,1,0:T(4,128)S(1)} %fusion.4, s32[]{:T(128)} %constant.43.clone.1), window={size=1x1x128 pad=0_0x0_0x127_0}, to_apply=%region_0.0 | reduce-window | flops 260096 | bytes 16388 | tf_op jit(solution)/shard_map/reduce-window
  11.5 0.2 slice_reduce_fusion
  11.7 0.2 reduce-window.9
  11.9 0.1 add_bitcast_fusion
  11.9 0.7 %fusion.3 = s32[512]{0:T(512)S(1)} fusion(s32[1,4,4,128]{3,2,1,0:T(4,128)S(1)} %add_bitcast_fusion, s32[512]{0:T(512)} %param.6), kind=kLoop, calls=%fused_computation.14 | loop fusion | flops 5632 | bytes 12288 | tf_op jit(solution)/shard_map/reduce_sum | solution.py:145
  12.6 0.7 %compare_select_fusion = s32[512]{0:T(512)S(1)} fusion(s32[512]{0:T(512)S(1)} %fusion.3, s32[512]{0:T(512)} %param.6, s32[]{:T(128)S(6)} %axis_index.23), kind=kLoop, calls=%fused_computation.20 | loop fusion | flops 9216 | bytes 6148 | tf_op jit(solution)/shard_map/select_n | solution.py:147
  13.3 2.3 %scatter_custom_fusion = bf16[1024,128]{1,0:T(8,128)(2,1)S(1)} fusion(s32[512]{0:T(512)S(1)} %compare_select_fusion, bf16[]{:T(256)} %constant.41.clone.1, bf16[512,128]{1,0:T(8,128)(2,1)} %param.4, f32[512]{0:T(512)} %param.5), kind=kCustom, calls=%fused_computation.10 | custom fusion | flops 196608 | bytes 395266 | tf_op jit(solution)/shard_map/scatter | solution.py:147
  15.6 2.2 %collective-permute-done.3 = bf16[1024,128]{1,0:T(8,128)(2,1)S(1)} collective-permute-done((bf16[1024,128]{1,0:T(8,128)(2,1)}, bf16[1024,128]{1,0:T(8,128)(2,1)S(1)}, u32[]{:S(2)}, u32[]{:S(2)}) %collective-permute-start.3) | collective-permute-done | bytes 262176 | tf_op jit(solution)/shard_map/ppermute | solution.py:116
  17.8 1.3 %collective-permute-start.4 = (bf16[1024,128]{1,0:T(8,128)(2,1)S(1)}, bf16[1024,128]{1,0:T(8,128)(2,1)S(1)}, u32[]{:S(2)}, u32[]{:S(2)}) collective-permute-start(bf16[1024,128]{1,0:T(8,128)(2,1)S(1)} %collective-permute-done.3), channel_id=1, source_target_pairs={{4,6},{5,7},{2,0},{3,1},{12,14},{13,15},{10,8},{11,9},{20,22},{21,... | collective-permute-start | bytes 786440 | tf_op jit(solution)/shard_map/ppermute | solution.py:116
  19.1 1.9 %collective-permute-start = (bf16[256,128]{1,0:T(8,128)(2,1)S(1)}, bf16[256,128]{1,0:T(8,128)(2,1)S(1)}, u32[]{:S(2)}, u32[]{:S(2)}) collective-permute-start(bf16[256,128]{1,0:T(8,128)(2,1)S(1)} %get-tuple-element.17), channel_id=1, source_target_pairs={{0,8},{8,16},{16,24},{24,0},{1,9},{9,17},{17,25},{25,1},{2,10},{10... | collective-permute-start | bytes 196616 | tf_op jit(solution)/shard_map/ppermute | solution.py:107
  21.0 1.5 %collective-permute-start.1 = (bf16[256,128]{1,0:T(8,128)(2,1)S(1)}, bf16[256,128]{1,0:T(8,128)(2,1)S(1)}, u32[]{:S(2)}, u32[]{:S(2)}) collective-permute-start(bf16[256,128]{1,0:T(8,128)(2,1)S(1)} %get-tuple-element.16), channel_id=1, source_target_pairs={{0,16},{8,24},{16,0},{24,8},{1,17},{9,25},{17,1},{25,9},{2,18},{10... | collective-permute-start | bytes 196616 | tf_op jit(solution)/shard_map/ppermute | solution.py:107
  22.5 1.8 %collective-permute-done = bf16[256,128]{1,0:T(8,128)(2,1)S(1)} collective-permute-done((bf16[256,128]{1,0:T(8,128)(2,1)S(1)}, bf16[256,128]{1,0:T(8,128)(2,1)S(1)}, u32[]{:S(2)}, u32[]{:S(2)}) %collective-permute-start) | collective-permute-done | bytes 65568 | tf_op jit(solution)/shard_map/ppermute | solution.py:107
  24.3 2.3 %collective-permute-start.2 = (bf16[256,128]{1,0:T(8,128)(2,1)S(1)}, bf16[256,128]{1,0:T(8,128)(2,1)S(1)}, u32[]{:S(2)}, u32[]{:S(2)}) collective-permute-start(bf16[256,128]{1,0:T(8,128)(2,1)S(1)} %get-tuple-element.15), channel_id=1, source_target_pairs={{0,24},{8,0},{16,8},{24,16},{1,25},{9,1},{17,9},{25,17},{2,26},{10... | collective-permute-start | bytes 196616 | tf_op jit(solution)/shard_map/ppermute | solution.py:107
  26.6 0.0 collective-permute-done.1
  26.6 0.0 copy-done.2
  26.6 0.0 collective-permute-start.9
  26.6 2.0 %collective-permute-done.2 = bf16[256,128]{1,0:T(8,128)(2,1)S(1)} collective-permute-done((bf16[256,128]{1,0:T(8,128)(2,1)S(1)}, bf16[256,128]{1,0:T(8,128)(2,1)S(1)}, u32[]{:S(2)}, u32[]{:S(2)}) %collective-permute-start.2) | collective-permute-done | bytes 65568 | tf_op jit(solution)/shard_map/ppermute | solution.py:107
  28.6 0.0 collective-permute-start.10
  28.6 0.0 collective-permute-done.5
  28.6 0.0 collective-permute-done.6
  28.6 0.0 collective-permute-done.4
  28.7 0.6 collective-permute-start.7
  29.3 0.1 collective-permute-start.8
  29.4 0.0 collective-permute-done.9
  29.4 0.8 %collective-permute-done.10 = bf16[1024,128]{1,0:T(8,128)(2,1)S(1)} collective-permute-done((bf16[1024,128]{1,0:T(8,128)(2,1)S(1)}, bf16[1024,128]{1,0:T(8,128)(2,1)S(1)}, u32[]{:S(2)}, u32[]{:S(2)}) %collective-permute-start.10) | collective-permute-done | bytes 262176 | tf_op jit(solution)/shard_map/ppermute | solution.py:130
  30.1 0.1 pad_maximum_fusion.1.refs_1_
  30.2 12.2 %shard_map.59 = (f32[1024,1]{1,0:T(8,128)S(1)}, f32[1024,1]{1,0:T(8,128)S(1)}, f32[1024,128]{1,0:T(8,128)S(1)}) custom-call(bf16[1024,128]{1,0:T(8,128)(2,1)S(1)} %pad_maximum_fusion.2.refs_0_, bf16[4096,128]{1,0:T(8,128)(2,1)S(1)} %pad_maximum_fusion.1.refs_1_), custom_call_target="tpu_custom_call" | custom-call | flops 2147483648 | bytes 1572864 | tf_op jit(solution)/shard_map/pallas_call | solution.py:83
  42.5 0.0 collective-permute-done.7
  42.5 0.0 collective-permute-done.8
  42.5 0.1 pad_maximum_fusion.refs_1_
  42.6 8.2 %shard_map.60 = bf16[1024,128]{1,0:T(8,128)(2,1)S(1)} custom-call(bf16[1024,128]{1,0:T(8,128)(2,1)S(1)} %pad_maximum_fusion.2.refs_0_, bf16[4096,128]{1,0:T(8,128)(2,1)S(1)} %pad_maximum_fusion.refs_1_, f32[1024,1]{1,0:T(8,128)S(1)} %get-tuple-element.5.refs_2_, f32[1024,1]{1,0:T(8,128)S(1)} %get-tuple-element.6.refs_3_, ...), custom_call_target="tpu_custom_call" | custom-call | flops 2147483648 | bytes 1572864 | tf_op jit(solution)/shard_map/pallas_call | solution.py:83
  50.7 0.0 copy-start.1
  50.8 0.0 copy-start.3
  50.8 3.2 %collective-permute-start.11 = (bf16[256,128]{1,0:T(8,128)(2,1)S(1)}, bf16[256,128]{1,0:T(8,128)(2,1)S(1)}, u32[]{:S(2)}, u32[]{:S(2)}) collective-permute-start(bf16[256,128]{1,0:T(8,128)(2,1)S(1)} %get-tuple-element.11), channel_id=1, source_target_pairs={{0,24},{8,0},{16,8},{24,16},{1,25},{9,1},{17,9},{25,17},{2,26},{10... | collective-permute-start | bytes 196616 | tf_op jit(solution)/shard_map/ppermute | solution.py:107
  54.0 0.1 collective-permute-start.12
  54.1 1.0 %collective-permute-start.13 = (bf16[256,128]{1,0:T(8,128)(2,1)S(1)}, bf16[256,128]{1,0:T(8,128)(2,1)S(1)}, u32[]{:S(2)}, u32[]{:S(2)}) collective-permute-start(bf16[256,128]{1,0:T(8,128)(2,1)S(1)} %get-tuple-element.9), channel_id=1, source_target_pairs={{0,8},{8,16},{16,24},{24,0},{1,9},{9,17},{17,25},{25,1},{2,10},{10... | collective-permute-start | bytes 196616 | tf_op jit(solution)/shard_map/ppermute | solution.py:107
  55.2 1.2 %collective-permute-done.11 = bf16[256,128]{1,0:T(8,128)(2,1)S(1)} collective-permute-done((bf16[256,128]{1,0:T(8,128)(2,1)S(1)}, bf16[256,128]{1,0:T(8,128)(2,1)S(1)}, u32[]{:S(2)}, u32[]{:S(2)}) %collective-permute-start.11) | collective-permute-done | bytes 65568 | tf_op jit(solution)/shard_map/ppermute | solution.py:107
  56.4 3.1 %collective-permute-done.12 = bf16[256,128]{1,0:T(8,128)(2,1)S(1)} collective-permute-done((bf16[256,128]{1,0:T(8,128)(2,1)S(1)}, bf16[256,128]{1,0:T(8,128)(2,1)S(1)}, u32[]{:S(2)}, u32[]{:S(2)}) %collective-permute-start.12) | collective-permute-done | bytes 65568 | tf_op jit(solution)/shard_map/ppermute | solution.py:107
  59.5 0.0 collective-permute-done.13
  59.5 1.3 %gather_fusion = bf16[512,128]{1,0:T(8,128)(2,1)S(1)} fusion(bf16[1024,128]{1,0:T(8,128)(2,1)S(1)} %pad_maximum_fusion.3, s32[1024]{0:T(1024)S(1)} %pad_clamp_fusion), kind=kCustom, calls=%fused_computation | custom fusion | bytes 264192 | tf_op jit(solution)/shard_map/gather | solution.py:155
  60.9 0.0 copy-done.1
  60.9 0.0 copy-done.3
  60.9 0.0 copy-start
  60.9 0.8 %subtract_convert_fusion = bf16[512,128]{1,0:T(8,128)(2,1)} fusion(bf16[512,128]{1,0:T(8,128)(2,1)S(1)} %gather_fusion, f32[512]{0:T(512)S(1)} %copy-done.3, bf16[512,128]{1,0:T(8,128)(2,1)S(1)} %copy-done.1), kind=kLoop, calls=%fused_computation.6 | loop fusion | flops 458752 | bytes 395264 | tf_op jit(solution)/shard_map/convert_element_type | solution.py:156
  61.7 0.0 copy-done
  (6 shorter events, 0.1 us)
Async XLA Ops:
  0.6 26.0 %copy-start.2 = (bf16[1024,128]{1,0:T(8,128)(2,1)S(1)}, bf16[1024,128]{1,0:T(8,128)(2,1)}, u32[]{:S(2)}) copy-start(bf16[1024,128]{1,0:T(8,128)(2,1)} %param.7) | copy-start | bytes 786436
  0.6 17.2 %collective-permute-start.3 = (bf16[1024,128]{1,0:T(8,128)(2,1)}, bf16[1024,128]{1,0:T(8,128)(2,1)S(1)}, u32[]{:S(2)}, u32[]{:S(2)}) collective-permute-start(bf16[1024,128]{1,0:T(8,128)(2,1)} %param.7), channel_id=1, source_target_pairs={{0,4},{1,5},{2,6},{3,7},{4,0},{5,1},{6,2},{7,3},{8,12},{9,13},{10,... | collective-permute-start | bytes 786440 | tf_op jit(solution)/shard_map/ppermute | solution.py:116
  4.8 23.9 %collective-permute-start.5 = (bf16[1024,128]{1,0:T(8,128)(2,1)}, bf16[1024,128]{1,0:T(8,128)(2,1)S(1)}, u32[]{:S(2)}, u32[]{:S(2)}) collective-permute-start(bf16[1024,128]{1,0:T(8,128)(2,1)} %param.7), channel_id=1, source_target_pairs={{0,2},{1,3},{2,4},{3,5},{4,6},{5,7},{8,10},{9,11},{10,12},{11,13},... | collective-permute-start | bytes 786440 | tf_op jit(solution)/shard_map/ppermute | solution.py:116
  8.3 20.4 %collective-permute-start.6 = (bf16[1024,128]{1,0:T(8,128)(2,1)}, bf16[1024,128]{1,0:T(8,128)(2,1)S(1)}, u32[]{:S(2)}, u32[]{:S(2)}) collective-permute-start(bf16[1024,128]{1,0:T(8,128)(2,1)} %param.7), channel_id=1, source_target_pairs={{2,0},{3,1},{4,2},{5,3},{6,4},{7,5},{10,8},{11,9},{12,10},{13,11},... | collective-permute-start | bytes 786440 | tf_op jit(solution)/shard_map/ppermute | solution.py:116
  17.8 10.8 %collective-permute-start.4 = (bf16[1024,128]{1,0:T(8,128)(2,1)S(1)}, bf16[1024,128]{1,0:T(8,128)(2,1)S(1)}, u32[]{:S(2)}, u32[]{:S(2)}) collective-permute-start(bf16[1024,128]{1,0:T(8,128)(2,1)S(1)} %collective-permute-done.3), channel_id=1, source_target_pairs={{4,6},{5,7},{2,0},{3,1},{12,14},{13,15},{10,8},{11,9},{20,22},{21,... | collective-permute-start | bytes 786440 | tf_op jit(solution)/shard_map/ppermute | solution.py:116
  19.1 5.2 %collective-permute-start = (bf16[256,128]{1,0:T(8,128)(2,1)S(1)}, bf16[256,128]{1,0:T(8,128)(2,1)S(1)}, u32[]{:S(2)}, u32[]{:S(2)}) collective-permute-start(bf16[256,128]{1,0:T(8,128)(2,1)S(1)} %get-tuple-element.17), channel_id=1, source_target_pairs={{0,8},{8,16},{16,24},{24,0},{1,9},{9,17},{17,25},{25,1},{2,10},{10... | collective-permute-start | bytes 196616 | tf_op jit(solution)/shard_map/ppermute | solution.py:107
  21.0 5.6 %collective-permute-start.1 = (bf16[256,128]{1,0:T(8,128)(2,1)S(1)}, bf16[256,128]{1,0:T(8,128)(2,1)S(1)}, u32[]{:S(2)}, u32[]{:S(2)}) collective-permute-start(bf16[256,128]{1,0:T(8,128)(2,1)S(1)} %get-tuple-element.16), channel_id=1, source_target_pairs={{0,16},{8,24},{16,0},{24,8},{1,17},{9,25},{17,1},{25,9},{2,18},{10... | collective-permute-start | bytes 196616 | tf_op jit(solution)/shard_map/ppermute | solution.py:107
  24.3 4.3 %collective-permute-start.2 = (bf16[256,128]{1,0:T(8,128)(2,1)S(1)}, bf16[256,128]{1,0:T(8,128)(2,1)S(1)}, u32[]{:S(2)}, u32[]{:S(2)}) collective-permute-start(bf16[256,128]{1,0:T(8,128)(2,1)S(1)} %get-tuple-element.15), channel_id=1, source_target_pairs={{0,24},{8,0},{16,8},{24,16},{1,25},{9,1},{17,9},{25,17},{2,26},{10... | collective-permute-start | bytes 196616 | tf_op jit(solution)/shard_map/ppermute | solution.py:107
  26.6 2.7 %collective-permute-start.9 = (bf16[1024,128]{1,0:T(8,128)(2,1)S(1)}, bf16[1024,128]{1,0:T(8,128)(2,1)S(1)}, u32[]{:S(2)}, u32[]{:S(2)}) collective-permute-start(bf16[1024,128]{1,0:T(8,128)(2,1)S(1)} %copy-done.2), channel_id=1, source_target_pairs={{0,1},{1,0},{2,3},{3,2},{4,5},{5,4},{6,7},{7,6},{8,9},{9,8},{10,11... | collective-permute-start | bytes 786440 | tf_op jit(solution)/shard_map/ppermute | solution.py:130
  28.6 1.5 %collective-permute-start.10 = (bf16[1024,128]{1,0:T(8,128)(2,1)S(1)}, bf16[1024,128]{1,0:T(8,128)(2,1)S(1)}, u32[]{:S(2)}, u32[]{:S(2)}) collective-permute-start(bf16[1024,128]{1,0:T(8,128)(2,1)S(1)} %collective-permute-done.3), channel_id=1, source_target_pairs={{0,1},{1,0},{2,3},{3,2},{4,5},{5,4},{6,7},{7,6},{8,9},{9,8},{10,11... | collective-permute-start | bytes 786440 | tf_op jit(solution)/shard_map/ppermute | solution.py:130
  28.7 13.7 %collective-permute-start.7 = (bf16[1024,128]{1,0:T(8,128)(2,1)S(1)}, bf16[1024,128]{1,0:T(8,128)(2,1)S(1)}, u32[]{:S(2)}, u32[]{:S(2)}) collective-permute-start(bf16[1024,128]{1,0:T(8,128)(2,1)S(1)} %get-tuple-element.12), channel_id=1, source_target_pairs={{0,1},{1,0},{2,3},{3,2},{4,5},{5,4},{6,7},{7,6},{8,9},{9,8},{10,11... | collective-permute-start | bytes 786440 | tf_op jit(solution)/shard_map/ppermute | solution.py:130
  29.3 13.2 %collective-permute-start.8 = (bf16[1024,128]{1,0:T(8,128)(2,1)S(1)}, bf16[1024,128]{1,0:T(8,128)(2,1)S(1)}, u32[]{:S(2)}, u32[]{:S(2)}) collective-permute-start(bf16[1024,128]{1,0:T(8,128)(2,1)S(1)} %get-tuple-element.13), channel_id=1, source_target_pairs={{0,1},{1,0},{2,3},{3,2},{4,5},{5,4},{6,7},{7,6},{8,9},{9,8},{10,11... | collective-permute-start | bytes 786440 | tf_op jit(solution)/shard_map/ppermute | solution.py:130
  50.7 10.1 %copy-start.1 = (bf16[512,128]{1,0:T(8,128)(2,1)S(1)}, bf16[512,128]{1,0:T(8,128)(2,1)}, u32[]{:S(2)}) copy-start(bf16[512,128]{1,0:T(8,128)(2,1)} %param.4) | copy-start | bytes 393220
  50.8 10.1 %copy-start.3 = (f32[512]{0:T(512)S(1)}, f32[512]{0:T(512)}, u32[]{:S(2)}) copy-start(f32[512]{0:T(512)} %param.5) | copy-start | bytes 6148
  50.8 5.6 %collective-permute-start.11 = (bf16[256,128]{1,0:T(8,128)(2,1)S(1)}, bf16[256,128]{1,0:T(8,128)(2,1)S(1)}, u32[]{:S(2)}, u32[]{:S(2)}) collective-permute-start(bf16[256,128]{1,0:T(8,128)(2,1)S(1)} %get-tuple-element.11), channel_id=1, source_target_pairs={{0,24},{8,0},{16,8},{24,16},{1,25},{9,1},{17,9},{25,17},{2,26},{10... | collective-permute-start | bytes 196616 | tf_op jit(solution)/shard_map/ppermute | solution.py:107
  54.0 5.5 %collective-permute-start.12 = (bf16[256,128]{1,0:T(8,128)(2,1)S(1)}, bf16[256,128]{1,0:T(8,128)(2,1)S(1)}, u32[]{:S(2)}, u32[]{:S(2)}) collective-permute-start(bf16[256,128]{1,0:T(8,128)(2,1)S(1)} %get-tuple-element.10), channel_id=1, source_target_pairs={{0,16},{8,24},{16,0},{24,8},{1,17},{9,25},{17,1},{25,9},{2,18},{10... | collective-permute-start | bytes 196616 | tf_op jit(solution)/shard_map/ppermute | solution.py:107
  54.1 5.4 %collective-permute-start.13 = (bf16[256,128]{1,0:T(8,128)(2,1)S(1)}, bf16[256,128]{1,0:T(8,128)(2,1)S(1)}, u32[]{:S(2)}, u32[]{:S(2)}) collective-permute-start(bf16[256,128]{1,0:T(8,128)(2,1)S(1)} %get-tuple-element.9), channel_id=1, source_target_pairs={{0,8},{8,16},{16,24},{24,0},{1,9},{9,17},{17,25},{25,1},{2,10},{10... | collective-permute-start | bytes 196616 | tf_op jit(solution)/shard_map/ppermute | solution.py:107
  60.9 0.8 %copy-start = (bf16[512,128]{1,0:T(8,128)(2,1)}, bf16[512,128]{1,0:T(8,128)(2,1)S(1)}, u32[]{:S(2)}) copy-start(bf16[512,128]{1,0:T(8,128)(2,1)S(1)} %gather_fusion) | copy-start | bytes 393220
